TPU v7x, 128 devices: a whole 4x4x4 slice. The times are simulated.
128 devices in a mesh: row: 4 (over z_hi, core), col: 4 (over y), rep: 8 (over x, z_lo).
Axes of the slice: x: 4, y: 4, z: 4 (z_hi: 2, z_lo: 2; z = z_hi * 2 + z_lo), core: 2. Of those that a mesh axis runs over, the one named last changes fastest.
Arguments:
- hidden: bfloat16 [8, 2048, 2048], P('rep', ('row', 'col')), may hold values from -6 to 6
- lengths: int32 [8, 4], P('rep'), may hold values from 1 to 1536, 2048 in all within a row
- prefix_latent: bfloat16 [2048, 576], P(('row', 'col', 'rep')), may hold values from -6 to 6
- gain_in: bfloat16 [2048], replicated, may hold values from 0.25 to 1.75
- query_weight: bfloat16 [2048, 1536], replicated, may hold values from -0.125 to 0.125
- latent_down: bfloat16 [2048, 576], replicated, may hold values from -0.125 to 0.125
- latent_gain: bfloat16 [512], replicated, may hold values from 0.25 to 1.75
- key_absorb: bfloat16 [8, 128, 512], replicated, may hold values from -8 to 8
- value_up: bfloat16 [8, 512, 128], replicated, may hold values from -0.25 to 0.25
- output_weight: bfloat16 [1024, 2048], replicated, may hold values from -0.5 to 0.5
- post_gain: bfloat16 [2048], replicated, may hold values from 0.25 to 1.75
- routes: int32 [8, 2048, 6], P('rep', ('row', 'col')), may hold values from 0 to 63, all different within a row; in each aligned block of 128 rows (0 to 127, 128 to 255, ..., all dimensions but the last counted through in order) at most 16 rows name the same one
- gate_weights: float32 [8, 2048, 6], P('rep', ('row', 'col')), may hold values from 0.1 to 1
- expert_gate_up: bfloat16 [128, 2048, 1408], P(('row', 'col', 'rep')), may hold values from -0.125 to 0.125
- expert_down: bfloat16 [128, 704, 2048], P(('row', 'col', 'rep')), may hold values from -0.15625 to 0.15625
Outputs:
- attended: bfloat16 [8, 2048, 2048], P('rep', ('row', 'col'))
- layer_out: bfloat16 [8, 2048, 2048], P('rep', ('row', 'col'))
Inputs may be any that keep to these rules, and one draw needn't show every extreme that they name: In each group the 4 lengths sum to 2048, and one of them is exactly 1536. `routes`: A token's 6 experts differ; among the 128 tokens of one device (aligned blocks of 128 tokens of a group) no expert is chosen more than 16 times, a bound that some block reaches.
All inputs are finite; a program needn't handle non-finite values.
Results may differ from a plain program's by a relative error of at most 0.014.
The roundings to bfloat16 on the way count: a program that leaves them out, or rounds other values in their place, can miss the bound.
Values may be sent and summed in bfloat16 or wider, within the bound.
No kernel may reach another device: no remote copies, remote signals or barrier semaphores. Data moves between devices by JAX's collectives and lax.ppermute only.
A program may use at most 128 MiB of HBM per device.

v0:
```python
import jax
import jax.numpy as jnp
from jax import lax
from jax.sharding import PartitionSpec as P

E = 64
CAP = 16


epsilon = 1e-06
rope_base = 50000.0
floor_value = -1e30


def rms_scale(values, gain_vector):
    mean_square = jnp.mean(values * values, axis=-1, keepdims=True)
    return values * lax.rsqrt(mean_square + epsilon) * gain_vector.astype(jnp.float32)


def rope_tables(positions, rope_width):
    halfway = rope_width // 2
    frequency = jnp.power(rope_base, -2.0 * jnp.arange(halfway, dtype=jnp.float32) / rope_width)
    angles = positions.astype(jnp.float32)[:, None] * frequency[None, :]
    return (jnp.cos(angles), jnp.sin(angles))


def rotate(values, cosine, sine_table):
    halfway = values.shape[-1] // 2
    leading = values[..., :halfway]
    trailing = values[..., halfway:]
    return jnp.concatenate(
        [leading * cosine - trailing * sine_table, trailing * cosine + leading * sine_table],
        axis=-1,
    )


def token_layout(group_lengths, first_place, row_count):
    ends = jnp.cumsum(group_lengths)
    starts = ends - group_lengths
    places = first_place + jnp.arange(row_count, dtype=jnp.int32)
    member = jnp.sum((places[:, None] >= ends[None, :]).astype(jnp.int32), axis=1)
    chosen = member[:, None] == jnp.arange(group_lengths.shape[0], dtype=jnp.int32)[None, :]
    offsets = jnp.sum(jnp.where(chosen, starts[None, :], 0), axis=1)
    return (member, places, places - offsets)


def make_queries(normed, positions, query_weight, latent_down, latent_gain, key_absorb):
    row_count = normed.shape[0]
    head_count = key_absorb.shape[0]
    plain_width = key_absorb.shape[1]
    latent_width = latent_gain.shape[0]
    projected = jnp.dot(normed, query_weight, preferred_element_type=jnp.float32).reshape(
        row_count, head_count, -1
    )
    rope_width = projected.shape[-1] - plain_width
    cosine, sine_table = rope_tables(positions, rope_width)
    query_plain = projected[..., :plain_width].astype(jnp.bfloat16)
    query_rotary = rotate(
        projected[..., plain_width:], cosine[:, None, :], sine_table[:, None, :]
    ).astype(jnp.bfloat16)
    query_latent = jnp.einsum(
        "thn,hnr->thr", query_plain, key_absorb, preferred_element_type=jnp.float32
    ).astype(jnp.bfloat16)
    query_rows = jnp.concatenate([query_latent, query_rotary], axis=-1)
    compressed = jnp.dot(normed, latent_down, preferred_element_type=jnp.float32)
    latent = rms_scale(compressed[:, :latent_width], latent_gain)
    key_rotary = rotate(compressed[:, latent_width:], cosine, sine_table)
    key_rows = jnp.concatenate([latent, key_rotary], axis=-1).astype(jnp.bfloat16)
    return (query_rows, key_rows)


def attend_block(state_now, query_rows, key_block, visible, scale_factor, latent_width):
    running_max, running_sum, weighted_sum = state_now
    scores = (
        lax.dot_general(
            query_rows, key_block, (((1,), (1,)), ((), ())), preferred_element_type=jnp.float32
        )
        * scale_factor
    )
    scores = jnp.where(visible, scores, -jnp.inf)
    new_max = jnp.maximum(running_max, jnp.max(scores, axis=1))
    rescale = jnp.exp(running_max - new_max)
    weights = jnp.exp(scores - new_max[:, None])
    running_sum = running_sum * rescale + jnp.sum(weights, axis=1)
    weighted_sum = weighted_sum * rescale[:, None] + jnp.dot(
        weights.astype(jnp.bfloat16),
        key_block[:, :latent_width],
        preferred_element_type=jnp.float32,
    )
    return (new_max, running_sum, weighted_sum)


def expert_apply(token_rows, expert_gate_up, expert_down):
    hidden_units = expert_down.shape[1]
    rows = token_rows.reshape(-1, token_rows.shape[-1])
    joint = jnp.dot(rows, expert_gate_up[0], preferred_element_type=jnp.float32)
    active = (jax.nn.silu(joint[:, :hidden_units]) * joint[:, hidden_units:]).astype(jnp.bfloat16)
    produced = jnp.dot(active, expert_down[0], preferred_element_type=jnp.float32)
    return produced.astype(jnp.bfloat16).reshape(token_rows.shape)


def gather_rows(rows, axes):
    count = lax.axis_size(axes)
    copies = jnp.broadcast_to(rows[None], (count,) + rows.shape)
    gathered = lax.all_to_all(copies, axes, split_axis=0, concat_axis=0, tiled=True)
    return gathered.reshape(count * rows.shape[0], rows.shape[1])


def on_device(
    hidden,
    lengths,
    prefix_latent,
    gain_in,
    query_weight,
    latent_down,
    latent_gain,
    key_absorb,
    value_up,
    output_weight,
    post_gain,
    routes,
    gate_weights,
    expert_gate_up,
    expert_down,
):
    token_count = hidden.shape[1]
    model_width = hidden.shape[2]
    head_count = key_absorb.shape[0]
    latent_width = latent_gain.shape[0]
    scale_factor = float(query_weight.shape[1] // head_count) ** (-0.5)
    group_lengths = lengths[0]
    prefix_total = prefix_latent.shape[0] * lax.axis_size(("row", "col", "rep"))
    first_place = lax.axis_index(("row", "col")) * token_count
    member, places, offsets = token_layout(group_lengths, first_place, token_count)
    own_tokens = hidden[0]
    normed = rms_scale(own_tokens.astype(jnp.float32), gain_in).astype(jnp.bfloat16)
    query_rows, key_rows = make_queries(
        normed, prefix_total + offsets, query_weight, latent_down, latent_gain, key_absorb
    )
    query_rows = query_rows.reshape(token_count * head_count, -1)
    row_member = jnp.repeat(member, head_count)
    row_places = jnp.repeat(places, head_count)
    row_total = token_count * head_count
    initial = (
        jnp.full((row_total,), floor_value, jnp.float32),
        jnp.zeros((row_total,), jnp.float32),
        jnp.zeros((row_total, latent_width), jnp.float32),
    )
    after_prefix = attend_block(
        initial,
        query_rows,
        gather_rows(prefix_latent, ("row", "col", "rep")),
        True,
        scale_factor,
        latent_width,
    )
    key_block = lax.all_gather(
        lax.all_gather(key_rows, "col", axis=0, tiled=True), "row", axis=0, tiled=True
    )
    block_member, block_places, block_offsets = token_layout(
        group_lengths, jnp.int32(0), key_block.shape[0]
    )
    visible = (row_member[:, None] == block_member[None, :]) & (
        row_places[:, None] >= block_places[None, :]
    )
    final_state = attend_block(
        after_prefix, query_rows, key_block, visible, scale_factor, latent_width
    )
    running_max, running_sum, weighted_sum = final_state
    mixed = (
        (weighted_sum / running_sum[:, None])
        .astype(jnp.bfloat16)
        .reshape(token_count, head_count, latent_width)
    )
    head_values = (
        jnp.einsum("thr,hrv->thv", mixed, value_up, preferred_element_type=jnp.float32)
        .astype(jnp.bfloat16)
        .reshape(token_count, -1)
    )
    attention = jnp.dot(head_values, output_weight, preferred_element_type=jnp.float32)
    residual = (own_tokens.astype(jnp.float32) + attention).astype(jnp.bfloat16)
    normed_post = rms_scale(residual.astype(jnp.float32), post_gain).astype(jnp.bfloat16)
    top_count = routes.shape[2]
    pair_count = token_count * top_count
    choices_flat = routes[0].reshape(-1)
    selected = (choices_flat[:, None] == jnp.arange(E, dtype=jnp.int32)[None, :]).astype(
        jnp.bfloat16
    )
    pair_ids = jnp.arange(pair_count, dtype=jnp.int32)
    lower = (pair_ids[:, None] >= pair_ids[None, :]).astype(jnp.bfloat16)
    running = jnp.dot(lower, selected, preferred_element_type=jnp.float32)
    slot_index = (
        jnp.sum(running * selected.astype(jnp.float32), axis=1).astype(jnp.int32) - 1
    )
    slot_place = choices_flat * CAP + slot_index
    pick_table = (
        slot_place[:, None] == jnp.arange(E * CAP, dtype=jnp.int32)[None, :]
    ).astype(jnp.bfloat16).reshape(token_count, top_count, E * CAP)
    occupancy = jnp.sum(pick_table, axis=1).reshape(token_count, E, 1, CAP)
    send_table = jnp.broadcast_to(occupancy, (token_count, E, 2, CAP)).reshape(token_count, -1)
    device_count = lax.axis_size(("row", "col", "rep"))
    per_device = expert_gate_up.shape[0]
    outgoing = (
        jnp.einsum("tj,td->jd", send_table, normed_post, preferred_element_type=jnp.float32)
        .astype(jnp.bfloat16)
        .reshape(device_count, per_device, CAP, model_width)
    )
    produced = expert_apply(
        lax.all_to_all(outgoing, ("row", "col", "rep"), split_axis=0, concat_axis=0, tiled=True),
        expert_gate_up,
        expert_down,
    )
    returned = lax.all_to_all(
        produced, ("row", "col", "rep"), split_axis=0, concat_axis=0, tiled=True
    )
    returned = returned.reshape(E, 2, CAP, model_width)
    picked_first = jnp.einsum(
        "tkp,pd->tkd",
        pick_table,
        returned[:, 0].reshape(E * CAP, model_width),
        preferred_element_type=jnp.float32,
    )
    picked_second = jnp.einsum(
        "tkp,pd->tkd",
        pick_table,
        returned[:, 1].reshape(E * CAP, model_width),
        preferred_element_type=jnp.float32,
    )
    picked = picked_first + picked_second
    mixture = jnp.sum(picked * gate_weights[0][:, :, None], axis=1)
    layer_out = (residual.astype(jnp.float32) + mixture).astype(jnp.bfloat16)
    return (attention.astype(jnp.bfloat16)[None], layer_out[None])


def solution(mesh):
    in_specs = (
        P("rep", ("row", "col"), None),
        P("rep", None),
        P(("row", "col", "rep"), None),
        P(),
        P(),
        P(),
        P(),
        P(),
        P(),
        P(),
        P(),
        P("rep", ("row", "col"), None),
        P("rep", ("row", "col"), None),
        P(("row", "col", "rep"), None, None),
        P(("row", "col", "rep"), None, None),
    )
    out_specs = (P("rep", ("row", "col"), None), P("rep", ("row", "col"), None))
    return jax.shard_map(
        on_device, mesh=mesh, in_specs=in_specs, out_specs=out_specs, check_vma=False
    )
```

profile of v0, /device:TPU:10, one launch (start us, length us, event | category | flops | bytes accessed | tf_op | source)
XLA Modules:
  0.0 394.3 jit_solution(4111171181203202752)
XLA Ops:
  7.3 1.0 reduce-window.4
  9.8 1.2 fusion.49
  11.0 2.7 fusion.65
  15.4 15.7 %all_gather.6 = bf16[512,576]{0,1:T(8,128)(2,1)} all-gather(bf16[128,576]{0,1:T(8,128)(2,1)S(1)} %pad_maximum_fusion.1), channel_id=1, replica_groups=mesh['row'=4,'col'=4,'rep'=8] {'col'}, dimensions={0}, use_global_device_ids=true | all-gather | bytes 737280 | tf_op jit(solution)/shard_map/all_gather | solution.py:158
  31.2 1.8 broadcast_in_dim.42
  33.0 10.5 %all-to-all-start = ((bf16[128,16,576]{2,1,0:T(8,128)(2,1)}), bf16[128,16,576]{2,1,0:T(8,128)(2,1)}, u32[]{:S(2)}, u32[]{:S(2)}) async-start(bf16[128,16,576]{2,1,0:T(8,128)(2,1)} %broadcast_in_dim.42), calls=%async_computation | async-start | bytes 5242880 | tf_op jit(solution)/shard_map/all_to_all | solution.py:105
  43.5 8.8 %copy.52 = bf16[2048,1536]{0,1:T(8,128)(2,1)} copy(bf16[2048,1536]{1,0:T(8,128)(2,1)} %param.19) | data formatting | bytes 12582912 | tf_op args[4]
  52.3 4.7 %fusion.63 = f32[128,8,192]{0,2,1:T(8,128)S(1)} fusion(bf16[8,192,2048]{2,1,0:T(8,128)(2,1)} %bitcast.102, bf16[1,128,2048]{2,1,0:T(8,128)(2,1)S(1)} %copy-done.2, f32[2048]{0:T(1024)S(1)} %convert_element_type.113, f32[128]{0:T(128)S(1)} %add_rsqrt_fusion.2), kind=kOutput, calls=%fused_computation.70 | convolution fusion | flops 806354944 | bytes 7610880 | tf_op jit(solution)/shard_map/dot_general | solution.py:52
  63.2 0.9 copy.61
  64.1 1.2 fusion.26
  65.3 1.8 copy.63
  68.5 1.9 fusion.33
  70.3 2.3 pad_maximum_fusion
  72.7 4.1 %all-to-all-done = bf16[128,16,576]{2,1,0:T(8,128)(2,1)} async-done(((bf16[128,16,576]{2,1,0:T(8,128)(2,1)}), bf16[128,16,576]{2,1,0:T(8,128)(2,1)}, u32[]{:S(2)}, u32[]{:S(2)}) %all-to-all-start) | async-done | bytes 2359328 | tf_op jit(solution)/shard_map/all_to_all | solution.py:105
  76.8 8.9 %multiply_reduce_fusion = (f32[1024]{0:T(1024)S(1)}, f32[1024,2048]{1,0:T(8,128)}) fusion(bf16[2048,576]{1,0:T(8,128)(2,1)} %bitcast.11, bf16[128,8,576]{2,0,1:T(8,128)(2,1)} %pad_maximum_fusion), kind=kOutput, calls=%fused_computation.5 | convolution fusion | flops 2420112384 | bytes 11931648 | tf_op jit(solution)/shard_map/dot_general | solution.py:75
  85.7 3.4 all-gather.2.cloned.1.call-done
  89.1 6.6 %fusion.81 = (f32[1024]{0:T(1024)S(1)}, f32[1024,2048]{1,0:T(8,128)S(1)}) fusion(bf16[2048,576]{0,1:T(8,128)(2,1)} %all-gather.2.cloned.1.call-done, bf16[128,8,576]{2,0,1:T(8,128)(2,1)} %pad_maximum_fusion, s32[1024]{0:T(1024)S(1)} %ge.63, s32[2048]{0:T(1024)S(1)} %convert_reduce_fusion, s32[1024]{0:T(1024)S(1)} %eq.86), kind=kOutput, calls=%fused_computation.116 | convolution fusion | flops 2428500992 | bytes 11948032 | tf_op jit(solution)/shard_map/dot_general | solution.py:75
  95.7 2.1 fusion.3
  97.8 4.0 %fusion.8 = f32[1024,512]{1,0:T(8,128)S(1)} fusion(f32[1024,2048]{1,0:T(8,128)S(1)} %copy-done.1, f32[1024]{0:T(1024)S(1)} %get-tuple-element.15, bf16[2048,576]{1,0:T(8,128)(2,1)} %bitcast.11), kind=kOutput, calls=%fused_computation.17 | convolution fusion | flops 2153775104 | bytes 12587008 | tf_op jit(solution)/shard_map/dot_general | solution.py:85
  101.8 1.3 fusion.1
  103.5 2.6 fusion.34
  107.0 1.6 fusion.55
  108.7 2.4 convolution_convert_fusion.1
  111.1 108.1 %all_to_all.15 = bf16[128,1,16,2048]{3,2,1,0:T(8,128)(2,1)S(1)} all-to-all(bf16[128,1,16,2048]{3,2,1,0:T(8,128)(2,1)S(1)} %bitcast.101), channel_id=1, replica_groups=mesh['row'=4,'col'=4,'rep'=8] {'row','col','rep'}, dimensions={0} | all-to-all | bytes 16777216 | tf_op jit(solution)/shard_map/all_to_all | solution.py:209
  219.2 17.8 %fusion.6 = f32[2048,1408]{0,1:T(8,128)} fusion(bf16[2048,2048]{1,0:T(8,128)(2,1)S(1)} %bitcast.104, bf16[1,2048,1408]{2,1,0:T(8,128)(2,1)} %param.28), kind=kOutput, calls=%fused_computation.15 | convolution fusion | flops 11811160064 | bytes 25690112 | tf_op jit(solution)/shard_map/dot_general | solution.py:96
  237.0 13.5 %convolution_convert_fusion = bf16[2048,2048]{1,0:T(8,128)(2,1)} fusion(f32[2048,1408]{0,1:T(8,128)} %fusion.6, bf16[1,704,2048]{2,1,0:T(8,128)(2,1)S(1)} %copy-done), kind=kOutput, calls=%fused_computation.6 | convolution fusion | flops 5918425088 | bytes 22806528 | tf_op jit(solution)/shard_map/dot_general | solution.py:98
  250.5 9.9 %all-to-all-start.2 = ((bf16[128,1,16,2048]{3,2,1,0:T(8,128)(2,1)}), bf16[128,1,16,2048]{3,2,1,0:T(8,128)(2,1)}, u32[]{:S(2)}, u32[]{:S(2)}) async-start(bf16[128,1,16,2048]{3,2,1,0:T(8,128)(2,1)} %bitcast.103), calls=%async_computation.2 | async-start | bytes 16777216 | tf_op jit(solution)/shard_map/all_to_all | solution.py:213
  260.5 114.2 %all-to-all-done.2 = bf16[128,1,16,2048]{3,2,1,0:T(8,128)(2,1)} async-done(((bf16[128,1,16,2048]{3,2,1,0:T(8,128)(2,1)}), bf16[128,1,16,2048]{3,2,1,0:T(8,128)(2,1)}, u32[]{:S(2)}, u32[]{:S(2)}) %all-to-all-start.2) | async-done | bytes 8388640 | tf_op jit(solution)/shard_map/all_to_all | solution.py:213
  374.7 4.0 %fusion.80 = (bf16[64,1,16,2048]{3,2,1,0:T(8,128)(2,1)S(1)}, bf16[64,1,16,2048]{3,2,1,0:T(8,128)(2,1)S(1)}) fusion(bf16[64,2,16,2048]{3,2,1,0:T(8,128)(2,1)} %bitcast.27), kind=kLoop, calls=%fused_computation.115 | loop fusion | bytes 16777216 | tf_op jit(solution)/shard_map/slice | solution.py:226
  378.7 3.5 fusion.17
  382.2 4.1 %multiply_reduce_fusion.1 = f32[128,2048]{1,0:T(8,128)S(1)} fusion(f32[128,6,2048]{2,0,1:T(8,128)S(1)} %fusion.17, bf16[1024,2048,1]{1,0,2:T(8,128)(2,1)S(1)} %bitcast.105, f32[128,6]{0,1:T(8,128)S(1)} %bitcast.110, s32[128,6]{0,1:T(8,128)S(1)} %copy.61), kind=kOutput, calls=%fused_computation.12 | convolution fusion | flops 3226468352 | bytes 11540480 | tf_op jit(solution)/shard_map/tkp,pd->tkd/dot_general | solution.py:223
  386.3 0.9 fusion.60
  (69 shorter events, 12.3 us)
Async XLA Ops:
  7.2 229.9 %copy-start = (bf16[1,704,2048]{2,1,0:T(8,128)(2,1)S(1)}, bf16[1,704,2048]{2,1,0:T(8,128)(2,1)}, u32[]{:S(2)}) copy-start(bf16[1,704,2048]{2,1,0:T(8,128)(2,1)} %param.29) | copy-start | bytes 8650756
  7.2 24.0 %copy-start.10 = (bf16[16,576]{1,0:T(8,128)(2,1)S(1)}, bf16[16,576]{1,0:T(8,128)(2,1)}, u32[]{:S(2)}) copy-start(bf16[16,576]{1,0:T(8,128)(2,1)} %param.17) | copy-start | bytes 55300
  7.2 81.9 %all-gather.2.cloned.1.call-start = ((), (), s32[]{:S(2)}) async-start(), calls=%async_computation.3 | async-start | bytes 2949120 | tf_op jit(solution)/shard_map/all_gather | solution.py:157
  7.3 25.7 %copy-start.12 = (s32[128]{0:T(128)}, s32[128]{0:T(128)S(1)}, u32[]{:S(2)}) copy-start(s32[128]{0:T(128)S(1)} %iota_add_fusion) | copy-start | bytes 1540
  8.3 24.7 %copy-start.14 = (s32[4,1]{0,1:T(1,128)}, s32[4,1]{0,1:T(1,128)S(1)}, u32[]{:S(2)}) copy-start(s32[4,1]{0,1:T(1,128)S(1)} %reduce-window.4) | copy-start | bytes 52
  9.0 24.0 %copy-start.13 = (s32[128]{0:T(128)}, s32[128]{0:T(128)S(1)}, u32[]{:S(2)}) copy-start(s32[128]{0:T(128)S(1)} %convert_reduce_fusion.1) | copy-start | bytes 1540
  33.0 43.8 %all-to-all-start = ((bf16[128,16,576]{2,1,0:T(8,128)(2,1)}), bf16[128,16,576]{2,1,0:T(8,128)(2,1)}, u32[]{:S(2)}, u32[]{:S(2)}) async-start(bf16[128,16,576]{2,1,0:T(8,128)(2,1)} %broadcast_in_dim.42), calls=%async_computation | async-start | bytes 5242880 | tf_op jit(solution)/shard_map/all_to_all | solution.py:105
  43.5 8.8 %copy-start.2 = (bf16[1,128,2048]{2,1,0:T(8,128)(2,1)S(1)}, bf16[1,128,2048]{2,1,0:T(8,128)(2,1)}, u32[]{:S(2)}) copy-start(bf16[1,128,2048]{2,1,0:T(8,128)(2,1)} %param.15) | copy-start | bytes 1572868
  52.3 5.6 %copy-start.9 = (f32[128,32]{0,1:T(8,128)S(1)}, f32[128,32]{0,1:T(8,128)}, u32[]{:S(2)}) copy-start(f32[128,32]{0,1:T(8,128)} %get-tuple-element.17) | copy-start | bytes 49156
  57.0 0.9 copy-start.6
  89.1 6.6 %copy-start.1 = (f32[1024,2048]{1,0:T(8,128)S(1)}, f32[1024,2048]{1,0:T(8,128)}, u32[]{:S(2)}) copy-start(f32[1024,2048]{1,0:T(8,128)} %get-tuple-element.21) | copy-start | bytes 25165828
  101.8 1.7 copy-start.15
  103.5 2.6 copy-start.8
  103.5 3.5 copy-start.5
  106.1 2.5 copy-start.7
  108.6 2.5 copy-start.3
  250.5 9.9 %copy-start.11 = (f32[1,128,6]{1,0,2:T(1,128)S(1)}, f32[1,128,6]{1,0,2:T(1,128)}, u32[]{:S(2)}) copy-start(f32[1,128,6]{1,0,2:T(1,128)} %param.27) | copy-start | bytes 9220
  250.5 124.1 %all-to-all-start.2 = ((bf16[128,1,16,2048]{3,2,1,0:T(8,128)(2,1)}), bf16[128,1,16,2048]{3,2,1,0:T(8,128)(2,1)}, u32[]{:S(2)}, u32[]{:S(2)}) async-start(bf16[128,1,16,2048]{3,2,1,0:T(8,128)(2,1)} %bitcast.103), calls=%async_computation.2 | async-start | bytes 16777216 | tf_op jit(solution)/shard_map/all_to_all | solution.py:213
  382.2 4.1 %copy-start.4 = (bf16[128,2048]{1,0:T(8,128)(2,1)S(1)}, bf16[128,2048]{1,0:T(8,128)(2,1)}, u32[]{:S(2)}) copy-start(bf16[128,2048]{1,0:T(8,128)(2,1)} %copy-done.3) | copy-start | bytes 1572868
Sparse Core Ops, SparseCore 0:
  31.3 57.7 all-gather.1
where the time goes:
time: 398 us; the launch traced here: 394 us
  blocking collectives  124 us (31%)
  waiting for transfers between devices  122 us (31%)
  matrix products  75.5 us (19%)
  local copies, waits for them, and re-layouts  22.9 us (6%)
  starting transfers between devices  20.4 us (5%)
  other arithmetic  15.3 us (4%)
  between operations  14.6 us (4%)
    all_to_all x1, waiting for transfers between devices, on_device(): lax.all_to_all(produced, ('row', 'col', 'rep'), split_axis=0, concat_axis...  114 us
    all_to_all x1, blocking collectives, on_device(): lax.all_to_all(outgoing, ('row', 'col', 'rep'), split_axis=0, concat_axis...  108 us
    dot_general x1, matrix products, expert_apply(): joint = jnp.dot(rows, expert_gate_up[0], preferred_element_type=jnp.float32)  17.8 us
    all_gather x1, blocking collectives, on_device(): lax.all_gather(key_rows, 'col', axis=0, tiled=True)  15.7 us
    dot_general x2, matrix products, attend_block(): lax.dot_general(query_rows, key_block, (((1,), (1,)), ((), ())), preferre...  15.5 us
    dot_general x1, matrix products, expert_apply(): jnp.dot(active, expert_down[0], preferred_element_type=jnp.float32)  13.5 us
    unnamed x35, local copies, waits for them, and re-layouts  10.9 us
    all_to_all x1, starting transfers between devices, gather_rows(): lax.all_to_all(copies, axes, split_axis=0, concat_axis=0, tiled=True)  10.5 us
  transfers between devices with their start and end apart: 3, of which 3 were waited for; matrix products, arithmetic and copies ran while one was open for 10% of the time, Pallas kernels for 0%

commit v1 on v0

--- a/solution.py
+++ b/solution.py
@@ -197,36 +197,44 @@
         slot_place[:, None] == jnp.arange(E * CAP, dtype=jnp.int32)[None, :]
     ).astype(jnp.bfloat16).reshape(token_count, top_count, E * CAP)
     occupancy = jnp.sum(pick_table, axis=1).reshape(token_count, E, 1, CAP)
-    send_table = jnp.broadcast_to(occupancy, (token_count, E, 2, CAP)).reshape(token_count, -1)
+    send_table = jnp.broadcast_to(occupancy, (token_count, E, 2, CAP))
+    pick_slots = pick_table.reshape(token_count, top_count, E, CAP)
     device_count = lax.axis_size(("row", "col", "rep"))
     per_device = expert_gate_up.shape[0]
-    outgoing = (
-        jnp.einsum("tj,td->jd", send_table, normed_post, preferred_element_type=jnp.float32)
-        .astype(jnp.bfloat16)
-        .reshape(device_count, per_device, CAP, model_width)
-    )
-    produced = expert_apply(
-        lax.all_to_all(outgoing, ("row", "col", "rep"), split_axis=0, concat_axis=0, tiled=True),
-        expert_gate_up,
-        expert_down,
-    )
-    returned = lax.all_to_all(
-        produced, ("row", "col", "rep"), split_axis=0, concat_axis=0, tiled=True
-    )
-    returned = returned.reshape(E, 2, CAP, model_width)
-    picked_first = jnp.einsum(
-        "tkp,pd->tkd",
-        pick_table,
-        returned[:, 0].reshape(E * CAP, model_width),
-        preferred_element_type=jnp.float32,
-    )
-    picked_second = jnp.einsum(
-        "tkp,pd->tkd",
-        pick_table,
-        returned[:, 1].reshape(E * CAP, model_width),
-        preferred_element_type=jnp.float32,
-    )
-    picked = picked_first + picked_second
+    chunk_count = 2
+    chunk = CAP // chunk_count
+    picked = None
+    for part in range(chunk_count):
+        window = slice(part * chunk, (part + 1) * chunk)
+        outgoing = (
+            jnp.einsum(
+                "tj,td->jd",
+                send_table[..., window].reshape(token_count, -1),
+                normed_post,
+                preferred_element_type=jnp.float32,
+            )
+            .astype(jnp.bfloat16)
+            .reshape(device_count, per_device, chunk, model_width)
+        )
+        produced = expert_apply(
+            lax.all_to_all(
+                outgoing, ("row", "col", "rep"), split_axis=0, concat_axis=0, tiled=True
+            ),
+            expert_gate_up,
+            expert_down,
+        )
+        returned = lax.all_to_all(
+            produced, ("row", "col", "rep"), split_axis=0, concat_axis=0, tiled=True
+        ).reshape(E, 2, chunk, model_width)
+        table = pick_slots[..., window].reshape(token_count, top_count, E * chunk)
+        for half in range(2):
+            term = jnp.einsum(
+                "tkp,pd->tkd",
+                table,
+                returned[:, half].reshape(E * chunk, model_width),
+                preferred_element_type=jnp.float32,
+            )
+            picked = term if picked is None else picked + term
     mixture = jnp.sum(picked * gate_weights[0][:, :, None], axis=1)
     layer_out = (residual.astype(jnp.float32) + mixture).astype(jnp.bfloat16)
     return (attention.astype(jnp.bfloat16)[None], layer_out[None])

time: 398 us -> 378 us (0.950)
  the two profiles are of different devices: /device:TPU:10 before, /device:TPU:1 now
where the time goes in v1:
time: 378 us; the launch traced here: 374 us
  waiting for transfers between devices  173 us (46%)
  matrix products  94.5 us (25%)
  starting transfers between devices  42.9 us (11%)
  local copies, waits for them, and re-layouts  19.9 us (5%)
  other arithmetic  15 us (4%)
  between operations  14.7 us (4%)
  blocking collectives  14.1 us (4%)
    all_to_all x2, waiting for transfers between devices, on_device(): lax.all_to_all(outgoing, ('row', 'col', 'rep'), split_axis=0, concat_axis...  85.4 us
    all_to_all x2, waiting for transfers between devices, on_device(): lax.all_to_all(produced, ('row', 'col', 'rep'), split_axis=0, concat_axis...  75.7 us
    dot_general x4, matrix products, on_device(): jnp.einsum('tkp,pd->tkd', table, returned[:, half].reshape(E * chunk, mod...  22.5 us
    dot_general x2, matrix products, expert_apply(): joint = jnp.dot(rows, expert_gate_up[0], preferred_element_type=jnp.float32)  20.9 us
    all_to_all x2, starting transfers between devices, on_device(): lax.all_to_all(outgoing, ('row', 'col', 'rep'), split_axis=0, concat_axis...  18.7 us
    dot_general x2, matrix products, attend_block(): lax.dot_general(query_rows, key_block, (((1,), (1,)), ((), ())), preferre...  15.5 us
    all_gather x1, blocking collectives, on_device(): lax.all_gather(key_rows, 'col', axis=0, tiled=True)  14.1 us
    unnamed x43, local copies, waits for them, and re-layouts  12.9 us
  transfers between devices with their start and end apart: 6, of which 6 were waited for; matrix products, arithmetic and copies ran while one was open for 22% of the time, Pallas kernels for 0%

profile of v1, /device:TPU:1, one launch (start us, length us, event | category | flops | bytes accessed | tf_op | source)
XLA Modules:
  0.0 373.9 jit_solution(7240920665498341728)
XLA Ops:
  11.7 2.7 fusion.69
  15.4 14.1 %all_gather.6 = bf16[512,576]{0,1:T(8,128)(2,1)} all-gather(bf16[128,576]{0,1:T(8,128)(2,1)S(1)} %pad_maximum_fusion.1), channel_id=1, replica_groups=mesh['row'=4,'col'=4,'rep'=8] {'col'}, dimensions={0}, use_global_device_ids=true | all-gather | bytes 737280 | tf_op jit(solution)/shard_map/all_gather | solution.py:158
  31.4 12.5 %all-to-all-start = ((bf16[128,16,576]{2,1,0:T(8,128)(2,1)}), bf16[128,16,576]{2,1,0:T(8,128)(2,1)}, u32[]{:S(2)}, u32[]{:S(2)}) async-start(bf16[128,16,576]{2,1,0:T(8,128)(2,1)} %broadcast_in_dim.44), calls=%async_computation | async-start | bytes 5242880 | tf_op jit(solution)/shard_map/all_to_all | solution.py:105
  47.6 9.2 %copy.68 = bf16[2048,1536]{0,1:T(8,128)(2,1)} copy(bf16[2048,1536]{1,0:T(8,128)(2,1)} %param.19) | data formatting | bytes 12582912 | tf_op args[4]
  56.9 4.7 %fusion.67 = f32[128,8,192]{0,2,1:T(8,128)S(1)} fusion(bf16[8,192,2048]{2,1,0:T(8,128)(2,1)} %bitcast.142, bf16[1,128,2048]{2,1,0:T(8,128)(2,1)S(1)} %copy-done.2, f32[2048]{0:T(1024)S(1)} %convert_element_type.122, f32[128]{0:T(128)S(1)} %add_rsqrt_fusion.2), kind=kOutput, calls=%fused_computation.85 | convolution fusion | flops 806354944 | bytes 7610880 | tf_op jit(solution)/shard_map/dot_general | solution.py:52
  64.9 1.9 fusion.38
  66.7 2.3 pad_maximum_fusion
  69.7 10.1 %all-to-all-done = bf16[128,16,576]{2,1,0:T(8,128)(2,1)} async-done(((bf16[128,16,576]{2,1,0:T(8,128)(2,1)}), bf16[128,16,576]{2,1,0:T(8,128)(2,1)}, u32[]{:S(2)}, u32[]{:S(2)}) %all-to-all-start) | async-done | bytes 2359328 | tf_op jit(solution)/shard_map/all_to_all | solution.py:105
  79.8 8.9 %multiply_reduce_fusion = (f32[1024]{0:T(1024)S(1)}, f32[1024,2048]{1,0:T(8,128)}) fusion(bf16[2048,576]{1,0:T(8,128)(2,1)} %bitcast.11, bf16[128,8,576]{2,0,1:T(8,128)(2,1)} %pad_maximum_fusion), kind=kOutput, calls=%fused_computation.5 | convolution fusion | flops 2420112384 | bytes 11931648 | tf_op jit(solution)/shard_map/dot_general | solution.py:75
  90.2 6.5 %fusion.86 = (f32[1024]{0:T(1024)S(1)}, f32[1024,2048]{1,0:T(8,128)S(1)}) fusion(bf16[2048,576]{0,1:T(8,128)(2,1)} %all-gather.2.cloned.1.call-done, bf16[128,8,576]{2,0,1:T(8,128)(2,1)} %pad_maximum_fusion, s32[1024]{0:T(1024)} %ge.63, s32[2048]{0:T(1024)} %convert_reduce_fusion, s32[1024]{0:T(1024)} %eq.73), kind=kOutput, calls=%fused_computation.131 | convolution fusion | flops 2428500992 | bytes 11948032 | tf_op jit(solution)/shard_map/dot_general | solution.py:75
  96.8 4.0 %fusion.9 = f32[1024,512]{1,0:T(8,128)S(1)} fusion(f32[1024,2048]{1,0:T(8,128)S(1)} %copy-done.1, f32[1024]{0:T(1024)S(1)} %get-tuple-element.15, bf16[2048,576]{1,0:T(8,128)(2,1)} %bitcast.11), kind=kOutput, calls=%fused_computation.15 | convolution fusion | flops 2153775104 | bytes 12587008 | tf_op jit(solution)/shard_map/dot_general | solution.py:85
  100.8 2.1 fusion.3
  104.6 2.6 fusion.39
  110.5 3.3 convert_bitcast_fusion.3
  113.7 12.7 %all-to-all-start.1 = ((bf16[128,1,8,2048]{3,2,1,0:T(8,128)(2,1)}), bf16[128,1,8,2048]{3,2,1,0:T(8,128)(2,1)}, u32[]{:S(2)}, u32[]{:S(2)}) async-start(bf16[128,1,8,2048]{3,2,1,0:T(8,128)(2,1)} %convert_bitcast_fusion.3), calls=%async_computation.1 | async-start | bytes 8388608 | tf_op jit(solution)/shard_map/all_to_all | solution.py:220
  126.5 3.3 convert_bitcast_fusion.1
  129.8 48.9 %all-to-all-done.1 = bf16[128,1,8,2048]{3,2,1,0:T(8,128)(2,1)} async-done(((bf16[128,1,8,2048]{3,2,1,0:T(8,128)(2,1)}), bf16[128,1,8,2048]{3,2,1,0:T(8,128)(2,1)}, u32[]{:S(2)}, u32[]{:S(2)}) %all-to-all-start.1) | async-done | bytes 4194336 | tf_op jit(solution)/shard_map/all_to_all | solution.py:220
  178.7 6.1 %all-to-all-start.3 = ((bf16[128,1,8,2048]{3,2,1,0:T(8,128)(2,1)}), bf16[128,1,8,2048]{3,2,1,0:T(8,128)(2,1)}, u32[]{:S(2)}, u32[]{:S(2)}) async-start(bf16[128,1,8,2048]{3,2,1,0:T(8,128)(2,1)} %convert_bitcast_fusion.1), calls=%async_computation.3 | async-start | bytes 8388608 | tf_op jit(solution)/shard_map/all_to_all | solution.py:220
  184.8 10.4 %fusion.7 = f32[1024,1408]{1,0:T(8,128)S(1)} fusion(bf16[1,2048,1408]{2,1,0:T(8,128)(2,1)} %param.28, bf16[128,1,8,2048]{3,2,1,0:T(8,128)(2,1)} %all-to-all-done.1), kind=kOutput, calls=%fused_computation.13 | convolution fusion | flops 5905580032 | bytes 15728640 | tf_op jit(solution)/shard_map/dot_general | solution.py:96
  195.3 5.2 %convert_bitcast_fusion.2 = bf16[128,1,8,2048]{3,2,1,0:T(8,128)(2,1)} fusion(bf16[1,704,2048]{2,1,0:T(8,128)(2,1)S(1)} %copy-done, f32[1024,1408]{1,0:T(8,128)S(1)} %fusion.7), kind=kOutput, calls=%fused_computation.21 | convolution fusion | flops 2959212544 | bytes 13369344 | tf_op jit(solution)/shard_map/dot_general | solution.py:98
  200.4 36.5 %all-to-all-done.3 = bf16[128,1,8,2048]{3,2,1,0:T(8,128)(2,1)} async-done(((bf16[128,1,8,2048]{3,2,1,0:T(8,128)(2,1)}), bf16[128,1,8,2048]{3,2,1,0:T(8,128)(2,1)}, u32[]{:S(2)}, u32[]{:S(2)}) %all-to-all-start.3) | async-done | bytes 4194336 | tf_op jit(solution)/shard_map/all_to_all | solution.py:220
  236.9 5.6 %all-to-all-start.2 = ((bf16[128,1,8,2048]{3,2,1,0:T(8,128)(2,1)}), bf16[128,1,8,2048]{3,2,1,0:T(8,128)(2,1)}, u32[]{:S(2)}, u32[]{:S(2)}) async-start(bf16[128,1,8,2048]{3,2,1,0:T(8,128)(2,1)} %convert_bitcast_fusion.2), calls=%async_computation.2 | async-start | bytes 8388608 | tf_op jit(solution)/shard_map/all_to_all | solution.py:226
  242.5 10.4 %fusion.5 = f32[1024,1408]{1,0:T(8,128)S(1)} fusion(bf16[1,2048,1408]{2,1,0:T(8,128)(2,1)} %param.28, bf16[128,1,8,2048]{3,2,1,0:T(8,128)(2,1)} %all-to-all-done.3), kind=kOutput, calls=%fused_computation.11 | convolution fusion | flops 5905580032 | bytes 15728640 | tf_op jit(solution)/shard_map/dot_general | solution.py:96
  253.0 5.2 %convert_bitcast_fusion = bf16[128,1,8,2048]{3,2,1,0:T(8,128)(2,1)} fusion(bf16[1,704,2048]{2,1,0:T(8,128)(2,1)S(1)} %copy-done, f32[1024,1408]{1,0:T(8,128)S(1)} %fusion.5), kind=kOutput, calls=%fused_computation.19 | convolution fusion | flops 2959212544 | bytes 13369344 | tf_op jit(solution)/shard_map/dot_general | solution.py:98
  258.2 36.6 %all-to-all-done.2 = bf16[128,1,8,2048]{3,2,1,0:T(8,128)(2,1)} async-done(((bf16[128,1,8,2048]{3,2,1,0:T(8,128)(2,1)}), bf16[128,1,8,2048]{3,2,1,0:T(8,128)(2,1)}, u32[]{:S(2)}, u32[]{:S(2)}) %all-to-all-start.2) | async-done | bytes 4194336 | tf_op jit(solution)/shard_map/all_to_all | solution.py:226
  294.8 6.1 %all-to-all-start.4 = ((bf16[128,1,8,2048]{3,2,1,0:T(8,128)(2,1)}), bf16[128,1,8,2048]{3,2,1,0:T(8,128)(2,1)}, u32[]{:S(2)}, u32[]{:S(2)}) async-start(bf16[128,1,8,2048]{3,2,1,0:T(8,128)(2,1)} %convert_bitcast_fusion), calls=%async_computation.4 | async-start | bytes 8388608 | tf_op jit(solution)/shard_map/all_to_all | solution.py:226
  301.5 6.4 %fusion.26 = f32[128,6,2048]{2,0,1:T(8,128)} fusion(bf16[64,2,8,2048]{3,2,1,0:T(8,128)(2,1)} %bitcast.27, pred[128,6,64,16]{0,3,2,1:T(8,128)(4,1)S(1)} %broadcast_compare_fusion), kind=kOutput, calls=%fused_computation.42 | convolution fusion | flops 1610612736 | bytes 8781824 | tf_op jit(solution)/shard_map/tkp,pd->tkd/dot_general | solution.py:231
  307.9 6.1 %fusion.25 = f32[128,6,2048]{2,0,1:T(8,128)} fusion(bf16[64,2,8,2048]{3,2,1,0:T(8,128)(2,1)} %bitcast.27, pred[128,6,64,16]{0,3,2,1:T(8,128)(4,1)S(1)} %broadcast_compare_fusion), kind=kOutput, calls=%fused_computation.40 | convolution fusion | flops 1610612736 | bytes 8781824 | tf_op jit(solution)/shard_map/tkp,pd->tkd/dot_general | solution.py:231
  314.0 39.1 %all-to-all-done.4 = bf16[128,1,8,2048]{3,2,1,0:T(8,128)(2,1)} async-done(((bf16[128,1,8,2048]{3,2,1,0:T(8,128)(2,1)}), bf16[128,1,8,2048]{3,2,1,0:T(8,128)(2,1)}, u32[]{:S(2)}, u32[]{:S(2)}) %all-to-all-start.4) | async-done | bytes 4194336 | tf_op jit(solution)/shard_map/all_to_all | solution.py:226
  353.1 3.8 %fusion.24 = f32[128,6,2048]{2,0,1:T(8,128)S(1)} fusion(bf16[64,2,8,2048]{3,2,1,0:T(8,128)(2,1)} %bitcast.39, pred[128,6,64,16]{0,3,2,1:T(8,128)(4,1)} %copy-done.9), kind=kOutput, calls=%fused_computation.38 | convolution fusion | flops 1610612736 | bytes 8781824 | tf_op jit(solution)/shard_map/tkp,pd->tkd/dot_general | solution.py:231
  358.4 6.2 %multiply_reduce_fusion.1 = f32[128,2048]{1,0:T(8,128)} fusion(f32[128,6,2048]{2,0,1:T(8,128)S(1)} %fusion.24, f32[128,6,2048]{2,0,1:T(8,128)S(1)} %copy-done.5, f32[128,6,2048]{2,0,1:T(8,128)S(1)} %copy-done.6, f32[128,6]{0,1:T(8,128)S(1)} %bitcast.147, bf16[64,2,8,2048]{3,2,1,0:T(8,128)(2,1)} %bitcast.39, pred[128,6,64,16]{0,3,2,1:T(8,128)(4,1)} %copy-done.9), kind=kOutput, calls=%fused_computation.10 | convolution fusion | flops 1618214912 | bytes 22416384 | tf_op jit(solution)/shard_map/tkp,pd->tkd/dot_general | solution.py:231
  364.6 2.1 fusion.65
  (90 shorter events, 23.4 us)
Async XLA Ops:
  7.2 188.1 %copy-start = (bf16[1,704,2048]{2,1,0:T(8,128)(2,1)S(1)}, bf16[1,704,2048]{2,1,0:T(8,128)(2,1)}, u32[]{:S(2)}) copy-start(bf16[1,704,2048]{2,1,0:T(8,128)(2,1)} %param.29) | copy-start | bytes 8650756
  7.2 22.4 %copy-start.15 = (bf16[16,576]{1,0:T(8,128)(2,1)S(1)}, bf16[16,576]{1,0:T(8,128)(2,1)}, u32[]{:S(2)}) copy-start(bf16[16,576]{1,0:T(8,128)(2,1)} %param.17) | copy-start | bytes 55300
  7.2 83.0 %all-gather.2.cloned.1.call-start = ((), (), s32[]{:S(2)}) async-start(), calls=%async_computation.5 | async-start | bytes 2949120 | tf_op jit(solution)/shard_map/all_gather | solution.py:157
  29.5 14.3 %copy-start.16 = (bf16[2048]{0:T(1024)(128)(2,1)S(1)}, bf16[2048]{0:T(1024)(128)(2,1)}, u32[]{:S(2)}) copy-start(bf16[2048]{0:T(1024)(128)(2,1)} %param.25) | copy-start | bytes 12292
  29.6 15.8 %copy-start.17 = (s32[1,128,6]{1,0,2:T(1,128)S(1)}, s32[1,128,6]{1,0,2:T(1,128)}, u32[]{:S(2)}) copy-start(s32[1,128,6]{1,0,2:T(1,128)} %param.26) | copy-start | bytes 9220
  31.4 48.4 %all-to-all-start = ((bf16[128,16,576]{2,1,0:T(8,128)(2,1)}), bf16[128,16,576]{2,1,0:T(8,128)(2,1)}, u32[]{:S(2)}, u32[]{:S(2)}) async-start(bf16[128,16,576]{2,1,0:T(8,128)(2,1)} %broadcast_in_dim.44), calls=%async_computation | async-start | bytes 5242880 | tf_op jit(solution)/shard_map/all_to_all | solution.py:105
  47.6 9.3 %copy-start.2 = (bf16[1,128,2048]{2,1,0:T(8,128)(2,1)S(1)}, bf16[1,128,2048]{2,1,0:T(8,128)(2,1)}, u32[]{:S(2)}) copy-start(bf16[1,128,2048]{2,1,0:T(8,128)(2,1)} %param.15) | copy-start | bytes 1572868
  56.9 5.6 %copy-start.13 = (f32[128,32]{0,1:T(8,128)S(1)}, f32[128,32]{0,1:T(8,128)}, u32[]{:S(2)}) copy-start(f32[128,32]{0,1:T(8,128)} %get-tuple-element.16) | copy-start | bytes 49156
  56.9 5.6 %copy-start.14 = (f32[128,32]{0,1:T(8,128)S(1)}, f32[128,32]{0,1:T(8,128)}, u32[]{:S(2)}) copy-start(f32[128,32]{0,1:T(8,128)} %get-tuple-element.17) | copy-start | bytes 49156
  61.6 0.9 copy-start.8
  64.2 4.9 %copy-start.11 = (bf16[128,1024]{0,1:T(8,128)(2,1)S(1)}, bf16[128,1024]{0,1:T(8,128)(2,1)}, u32[]{:S(2)}) copy-start(bf16[128,1024]{0,1:T(8,128)(2,1)} %copy.79) | copy-start | bytes 786436
  90.2 6.6 %copy-start.1 = (f32[1024,2048]{1,0:T(8,128)S(1)}, f32[1024,2048]{1,0:T(8,128)}, u32[]{:S(2)}) copy-start(f32[1024,2048]{1,0:T(8,128)} %get-tuple-element.21) | copy-start | bytes 25165828
  102.9 1.7 copy-start.19
  104.6 2.6 copy-start.10
  104.6 3.5 copy-start.7
  107.2 2.5 copy-start.12
  109.7 0.8 copy-start.3
  113.7 12.7 %copy-start.4 = (bf16[128,2048]{1,0:T(8,128)(2,1)S(1)}, bf16[128,2048]{1,0:T(8,128)(2,1)}, u32[]{:S(2)}) copy-start(bf16[128,2048]{1,0:T(8,128)(2,1)} %copy-done.3) | copy-start | bytes 1572868
  113.7 65.0 %all-to-all-start.1 = ((bf16[128,1,8,2048]{3,2,1,0:T(8,128)(2,1)}), bf16[128,1,8,2048]{3,2,1,0:T(8,128)(2,1)}, u32[]{:S(2)}, u32[]{:S(2)}) async-start(bf16[128,1,8,2048]{3,2,1,0:T(8,128)(2,1)} %convert_bitcast_fusion.3), calls=%async_computation.1 | async-start | bytes 8388608 | tf_op jit(solution)/shard_map/all_to_all | solution.py:220
  178.7 58.2 %all-to-all-start.3 = ((bf16[128,1,8,2048]{3,2,1,0:T(8,128)(2,1)}), bf16[128,1,8,2048]{3,2,1,0:T(8,128)(2,1)}, u32[]{:S(2)}, u32[]{:S(2)}) async-start(bf16[128,1,8,2048]{3,2,1,0:T(8,128)(2,1)} %convert_bitcast_fusion.1), calls=%async_computation.3 | async-start | bytes 8388608 | tf_op jit(solution)/shard_map/all_to_all | solution.py:220
  236.9 57.9 %all-to-all-start.2 = ((bf16[128,1,8,2048]{3,2,1,0:T(8,128)(2,1)}), bf16[128,1,8,2048]{3,2,1,0:T(8,128)(2,1)}, u32[]{:S(2)}, u32[]{:S(2)}) async-start(bf16[128,1,8,2048]{3,2,1,0:T(8,128)(2,1)} %convert_bitcast_fusion.2), calls=%async_computation.2 | async-start | bytes 8388608 | tf_op jit(solution)/shard_map/all_to_all | solution.py:226
  258.2 42.7 %copy-start.18 = (f32[1,128,6]{1,0,2:T(1,128)S(1)}, f32[1,128,6]{1,0,2:T(1,128)}, u32[]{:S(2)}) copy-start(f32[1,128,6]{1,0,2:T(1,128)} %param.27) | copy-start | bytes 9220
  294.8 58.2 %all-to-all-start.4 = ((bf16[128,1,8,2048]{3,2,1,0:T(8,128)(2,1)}), bf16[128,1,8,2048]{3,2,1,0:T(8,128)(2,1)}, u32[]{:S(2)}, u32[]{:S(2)}) async-start(bf16[128,1,8,2048]{3,2,1,0:T(8,128)(2,1)} %convert_bitcast_fusion), calls=%async_computation.4 | async-start | bytes 8388608 | tf_op jit(solution)/shard_map/all_to_all | solution.py:226
  301.5 6.4 %copy-start.9 = (pred[128,6,64,16]{0,3,2,1:T(8,128)(4,1)}, pred[128,6,64,16]{0,3,2,1:T(8,128)(4,1)S(1)}, u32[]{:S(2)}) copy-start(pred[128,6,64,16]{0,3,2,1:T(8,128)(4,1)S(1)} %broadcast_compare_fusion) | copy-start | bytes 2359300
  353.1 3.8 %copy-start.5 = (f32[128,6,2048]{2,0,1:T(8,128)S(1)}, f32[128,6,2048]{2,0,1:T(8,128)}, u32[]{:S(2)}) copy-start(f32[128,6,2048]{2,0,1:T(8,128)} %fusion.26) | copy-start | bytes 18874372
  353.1 5.4 %copy-start.6 = (f32[128,6,2048]{2,0,1:T(8,128)S(1)}, f32[128,6,2048]{2,0,1:T(8,128)}, u32[]{:S(2)}) copy-start(f32[128,6,2048]{2,0,1:T(8,128)} %fusion.25) | copy-start | bytes 18874372
Sparse Core Ops, SparseCore 0:
  29.7 60.4 all-gather.1

commit v2 on v1

--- a/solution.py
+++ b/solution.py
@@ -203,7 +203,10 @@
     per_device = expert_gate_up.shape[0]
     chunk_count = 2
     chunk = CAP // chunk_count
-    picked = None
+    gate_table = jnp.sum(
+        pick_slots.astype(jnp.float32) * gate_weights[0][:, :, None, None], axis=1
+    )
+    mixture = None
     for part in range(chunk_count):
         window = slice(part * chunk, (part + 1) * chunk)
         outgoing = (
@@ -226,16 +229,14 @@
         returned = lax.all_to_all(
             produced, ("row", "col", "rep"), split_axis=0, concat_axis=0, tiled=True
         ).reshape(E, 2, chunk, model_width)
-        table = pick_slots[..., window].reshape(token_count, top_count, E * chunk)
-        for half in range(2):
-            term = jnp.einsum(
-                "tkp,pd->tkd",
-                table,
-                returned[:, half].reshape(E * chunk, model_width),
-                preferred_element_type=jnp.float32,
-            )
-            picked = term if picked is None else picked + term
-    mixture = jnp.sum(picked * gate_weights[0][:, :, None], axis=1)
+        paired = returned[:, 0].astype(jnp.float32) + returned[:, 1].astype(jnp.float32)
+        term = jnp.dot(
+            gate_table[..., window].reshape(token_count, E * chunk),
+            paired.reshape(E * chunk, model_width),
+            precision=lax.Precision.HIGHEST,
+            preferred_element_type=jnp.float32,
+        )
+        mixture = term if mixture is None else mixture + term
     layer_out = (residual.astype(jnp.float32) + mixture).astype(jnp.bfloat16)
     return (attention.astype(jnp.bfloat16)[None], layer_out[None])
 

time: 378 us -> 378 us (level)
  matrix products: 94.5 us -> 82.4 us
  other arithmetic: 15 us -> 23.5 us
    dot_general x4 -> x2, matrix products: 22.5 us -> 10.3 us  [on_device(): jnp.dot(gate_table[..., window].reshape(token_count, E * chunk), paired.r...]
    add x0 -> x2, other arithmetic: none -> 8.06 us  [on_device(): returned[:, 0].astype(jnp.float32) + returned[:, 1].astype(jnp.float32)]
    all_to_all x2, waiting for transfers between devices: 75.7 us -> 82.4 us  [on_device(): lax.all_to_all(produced, ('row', 'col', 'rep'), split_axis=0, concat_axis...]
    all_to_all x1, waiting for transfers between devices: 10.1 us -> 4.07 us  [gather_rows(): lax.all_to_all(copies, axes, split_axis=0, concat_axis=0, tiled=True)]
where the time goes in v2:
time: 378 us; the launch traced here: 375 us
  waiting for transfers between devices  174 us (46%)
  matrix products  82.4 us (22%)
  starting transfers between devices  44.3 us (12%)
  other arithmetic  23.5 us (6%)
  local copies, waits for them, and re-layouts  22.4 us (6%)
  between operations  14.6 us (4%)
  blocking collectives  14.1 us (4%)
    all_to_all x2, waiting for transfers between devices, on_device(): lax.all_to_all(outgoing, ('row', 'col', 'rep'), split_axis=0, concat_axis...  85.5 us
    all_to_all x2, waiting for transfers between devices, on_device(): lax.all_to_all(produced, ('row', 'col', 'rep'), split_axis=0, concat_axis...  82.4 us
    dot_general x2, matrix products, expert_apply(): joint = jnp.dot(rows, expert_gate_up[0], preferred_element_type=jnp.float32)  20.9 us
    all_to_all x2, starting transfers between devices, on_device(): lax.all_to_all(outgoing, ('row', 'col', 'rep'), split_axis=0, concat_axis...  19.8 us
    dot_general x2, matrix products, attend_block(): lax.dot_general(query_rows, key_block, (((1,), (1,)), ((), ())), preferre...  15.5 us
    all_gather x1, blocking collectives, on_device(): lax.all_gather(key_rows, 'col', axis=0, tiled=True)  14.1 us
    all_to_all x1, starting transfers between devices, gather_rows(): lax.all_to_all(copies, axes, split_axis=0, concat_axis=0, tiled=True)  12.8 us
    unnamed x43, local copies, waits for them, and re-layouts  11.7 us
  transfers between devices with their start and end apart: 6, of which 6 were waited for; matrix products, arithmetic and copies ran while one was open for 22% of the time, Pallas kernels for 0%

profile of v2, /device:TPU:1, one launch (start us, length us, event | category | flops | bytes accessed | tf_op | source)
XLA Modules:
  0.0 375.0 jit_solution(381734676270379463)
XLA Ops:
  11.0 2.7 fusion.86
  15.4 14.1 %all_gather.6 = bf16[512,576]{0,1:T(8,128)(2,1)} all-gather(bf16[128,576]{0,1:T(8,128)(2,1)S(1)} %pad_maximum_fusion.1), channel_id=1, replica_groups=mesh['row'=4,'col'=4,'rep'=8] {'col'}, dimensions={0}, use_global_device_ids=true | all-gather | bytes 737280 | tf_op jit(solution)/shard_map/all_gather | solution.py:158
  31.4 12.8 %all-to-all-start = ((bf16[128,16,576]{2,1,0:T(8,128)(2,1)}), bf16[128,16,576]{2,1,0:T(8,128)(2,1)}, u32[]{:S(2)}, u32[]{:S(2)}) async-start(bf16[128,16,576]{2,1,0:T(8,128)(2,1)} %broadcast_in_dim.44), calls=%async_computation | async-start | bytes 5242880 | tf_op jit(solution)/shard_map/all_to_all | solution.py:105
  44.2 8.8 %copy.54 = bf16[2048,1536]{0,1:T(8,128)(2,1)} copy(bf16[2048,1536]{1,0:T(8,128)(2,1)} %param.19) | data formatting | bytes 12582912 | tf_op args[4]
  53.1 4.7 %fusion.84 = f32[128,8,192]{0,2,1:T(8,128)S(1)} fusion(bf16[8,192,2048]{2,1,0:T(8,128)(2,1)} %bitcast.122, bf16[1,128,2048]{2,1,0:T(8,128)(2,1)S(1)} %copy-done.3, f32[2048]{0:T(1024)S(1)} %convert_element_type.144, f32[128]{0:T(128)S(1)} %add_rsqrt_fusion.2), kind=kOutput, calls=%fused_computation.85 | convolution fusion | flops 806354944 | bytes 7610880 | tf_op jit(solution)/shard_map/dot_general | solution.py:52
  67.3 1.8 copy.66
  71.1 1.9 fusion.57
  72.9 2.3 pad_maximum_fusion
  75.9 4.1 %all-to-all-done = bf16[128,16,576]{2,1,0:T(8,128)(2,1)} async-done(((bf16[128,16,576]{2,1,0:T(8,128)(2,1)}), bf16[128,16,576]{2,1,0:T(8,128)(2,1)}, u32[]{:S(2)}, u32[]{:S(2)}) %all-to-all-start) | async-done | bytes 2359328 | tf_op jit(solution)/shard_map/all_to_all | solution.py:105
  80.0 8.9 %multiply_reduce_fusion = (f32[1024]{0:T(1024)S(1)}, f32[1024,2048]{1,0:T(8,128)}) fusion(bf16[2048,576]{1,0:T(8,128)(2,1)} %bitcast.11, bf16[128,8,576]{2,0,1:T(8,128)(2,1)} %pad_maximum_fusion), kind=kOutput, calls=%fused_computation.5 | convolution fusion | flops 2420112384 | bytes 11931648 | tf_op jit(solution)/shard_map/dot_general | solution.py:75
  90.5 6.5 %fusion.106 = (f32[1024]{0:T(1024)S(1)}, f32[1024,2048]{1,0:T(8,128)S(1)}) fusion(bf16[2048,576]{0,1:T(8,128)(2,1)} %all-gather.2.cloned.1.call-done, bf16[128,8,576]{2,0,1:T(8,128)(2,1)} %pad_maximum_fusion, s32[1024]{0:T(1024)} %ge.63, s32[2048]{0:T(1024)} %convert_reduce_fusion, s32[1024]{0:T(1024)} %eq.73), kind=kOutput, calls=%fused_computation.134 | convolution fusion | flops 2428500992 | bytes 11948032 | tf_op jit(solution)/shard_map/dot_general | solution.py:75
  97.1 2.1 fusion.3
  99.3 4.0 %fusion.9 = f32[1024,512]{1,0:T(8,128)S(1)} fusion(f32[1024,2048]{1,0:T(8,128)S(1)} %copy-done.2, f32[1024]{0:T(1024)S(1)} %get-tuple-element.17, bf16[2048,576]{1,0:T(8,128)(2,1)} %bitcast.11), kind=kOutput, calls=%fused_computation.14 | convolution fusion | flops 2153775104 | bytes 12587008 | tf_op jit(solution)/shard_map/dot_general | solution.py:85
  105.0 2.6 fusion.58
  110.8 3.3 convert_bitcast_fusion.1
  114.1 13.6 %all-to-all-start.3 = ((bf16[128,1,8,2048]{3,2,1,0:T(8,128)(2,1)}), bf16[128,1,8,2048]{3,2,1,0:T(8,128)(2,1)}, u32[]{:S(2)}, u32[]{:S(2)}) async-start(bf16[128,1,8,2048]{3,2,1,0:T(8,128)(2,1)} %convert_bitcast_fusion.1), calls=%async_computation.3 | async-start | bytes 8388608 | tf_op jit(solution)/shard_map/all_to_all | solution.py:223
  127.8 3.3 convert_bitcast_fusion.3
  131.0 49.0 %all-to-all-done.3 = bf16[128,1,8,2048]{3,2,1,0:T(8,128)(2,1)} async-done(((bf16[128,1,8,2048]{3,2,1,0:T(8,128)(2,1)}), bf16[128,1,8,2048]{3,2,1,0:T(8,128)(2,1)}, u32[]{:S(2)}, u32[]{:S(2)}) %all-to-all-start.3) | async-done | bytes 4194336 | tf_op jit(solution)/shard_map/all_to_all | solution.py:223
  180.0 6.2 %all-to-all-start.1 = ((bf16[128,1,8,2048]{3,2,1,0:T(8,128)(2,1)}), bf16[128,1,8,2048]{3,2,1,0:T(8,128)(2,1)}, u32[]{:S(2)}, u32[]{:S(2)}) async-start(bf16[128,1,8,2048]{3,2,1,0:T(8,128)(2,1)} %convert_bitcast_fusion.3), calls=%async_computation.1 | async-start | bytes 8388608 | tf_op jit(solution)/shard_map/all_to_all | solution.py:223
  186.3 10.4 %fusion.5 = f32[1024,1408]{1,0:T(8,128)S(1)} fusion(bf16[1,2048,1408]{2,1,0:T(8,128)(2,1)} %param.28, bf16[128,1,8,2048]{3,2,1,0:T(8,128)(2,1)} %all-to-all-done.3), kind=kOutput, calls=%fused_computation.10 | convolution fusion | flops 5905580032 | bytes 15728640 | tf_op jit(solution)/shard_map/dot_general | solution.py:96
  196.7 5.2 %convert_bitcast_fusion = bf16[128,1,8,2048]{3,2,1,0:T(8,128)(2,1)} fusion(bf16[1,704,2048]{2,1,0:T(8,128)(2,1)S(1)} %copy-done, f32[1024,1408]{1,0:T(8,128)S(1)} %fusion.5), kind=kOutput, calls=%fused_computation.23 | convolution fusion | flops 2959212544 | bytes 13369344 | tf_op jit(solution)/shard_map/dot_general | solution.py:98
  201.9 36.5 %all-to-all-done.1 = bf16[128,1,8,2048]{3,2,1,0:T(8,128)(2,1)} async-done(((bf16[128,1,8,2048]{3,2,1,0:T(8,128)(2,1)}), bf16[128,1,8,2048]{3,2,1,0:T(8,128)(2,1)}, u32[]{:S(2)}, u32[]{:S(2)}) %all-to-all-start.1) | async-done | bytes 4194336 | tf_op jit(solution)/shard_map/all_to_all | solution.py:223
  238.4 5.6 %all-to-all-start.4 = ((bf16[128,1,8,2048]{3,2,1,0:T(8,128)(2,1)}), bf16[128,1,8,2048]{3,2,1,0:T(8,128)(2,1)}, u32[]{:S(2)}, u32[]{:S(2)}) async-start(bf16[128,1,8,2048]{3,2,1,0:T(8,128)(2,1)} %convert_bitcast_fusion), calls=%async_computation.4 | async-start | bytes 8388608 | tf_op jit(solution)/shard_map/all_to_all | solution.py:229
  244.0 10.4 %fusion.7 = f32[1024,1408]{1,0:T(8,128)S(1)} fusion(bf16[1,2048,1408]{2,1,0:T(8,128)(2,1)} %param.28, bf16[128,1,8,2048]{3,2,1,0:T(8,128)(2,1)} %all-to-all-done.1), kind=kOutput, calls=%fused_computation.12 | convolution fusion | flops 5905580032 | bytes 15728640 | tf_op jit(solution)/shard_map/dot_general | solution.py:96
  254.5 5.2 %convert_bitcast_fusion.2 = bf16[128,1,8,2048]{3,2,1,0:T(8,128)(2,1)} fusion(bf16[1,704,2048]{2,1,0:T(8,128)(2,1)S(1)} %copy-done, f32[1024,1408]{1,0:T(8,128)S(1)} %fusion.7), kind=kOutput, calls=%fused_computation.26 | convolution fusion | flops 2959212544 | bytes 13369344 | tf_op jit(solution)/shard_map/dot_general | solution.py:98
  259.7 36.6 %all-to-all-done.4 = bf16[128,1,8,2048]{3,2,1,0:T(8,128)(2,1)} async-done(((bf16[128,1,8,2048]{3,2,1,0:T(8,128)(2,1)}), bf16[128,1,8,2048]{3,2,1,0:T(8,128)(2,1)}, u32[]{:S(2)}, u32[]{:S(2)}) %all-to-all-start.4) | async-done | bytes 4194336 | tf_op jit(solution)/shard_map/all_to_all | solution.py:229
  296.3 6.0 %all-to-all-start.2 = ((bf16[128,1,8,2048]{3,2,1,0:T(8,128)(2,1)}), bf16[128,1,8,2048]{3,2,1,0:T(8,128)(2,1)}, u32[]{:S(2)}, u32[]{:S(2)}) async-start(bf16[128,1,8,2048]{3,2,1,0:T(8,128)(2,1)} %convert_bitcast_fusion.2), calls=%async_computation.2 | async-start | bytes 8388608 | tf_op jit(solution)/shard_map/all_to_all | solution.py:229
  303.7 5.0 %add_bitcast_fusion = f32[64,8,2048]{2,1,0:T(8,128)} fusion(bf16[64,2,8,2048]{3,2,1,0:T(8,128)(2,1)} %bitcast.35), kind=kLoop, calls=%fused_computation.22 | loop fusion | flops 3145728 | bytes 8388608 | tf_op jit(solution)/shard_map/add | solution.py:232
  308.7 45.8 %all-to-all-done.2 = bf16[128,1,8,2048]{3,2,1,0:T(8,128)(2,1)} async-done(((bf16[128,1,8,2048]{3,2,1,0:T(8,128)(2,1)}), bf16[128,1,8,2048]{3,2,1,0:T(8,128)(2,1)}, u32[]{:S(2)}, u32[]{:S(2)}) %all-to-all-start.2) | async-done | bytes 4194336 | tf_op jit(solution)/shard_map/all_to_all | solution.py:229
  354.5 3.1 add_bitcast_fusion.1
  357.6 4.7 %fusion.27 = f32[128,2048]{1,0:T(8,128)S(1)} fusion(f32[64,8,2048]{2,1,0:T(8,128)S(1)} %add_bitcast_fusion.1, f32[128,64,8]{0,2,1:T(8,128)S(1)} %copy-done.11), kind=kOutput, calls=%fused_computation.41 | convolution fusion | flops 1610612736 | bytes 5505024 | tf_op jit(solution)/shard_map/dot_general | solution.py:233
  362.3 5.6 %fusion.43 = bf16[1,128,2048]{2,1,0:T(8,128)(2,1)} fusion(f32[128,2048]{1,0:T(8,128)S(1)} %fusion.27, f32[64,8,2048]{2,1,0:T(8,128)S(1)} %copy-done.1, bf16[128,2048]{1,0:T(8,128)(2,1)S(1)} %copy-done.5, f32[128,64,8]{0,2,1:T(8,128)S(1)} %copy-done.9), kind=kOutput, calls=%fused_computation.48 | convolution fusion | flops 1611661312 | bytes 6553600 | tf_op jit(solution)/shard_map/dot_general | solution.py:233
  (90 shorter events, 27.3 us)
Async XLA Ops:
  7.2 189.6 %copy-start = (bf16[1,704,2048]{2,1,0:T(8,128)(2,1)S(1)}, bf16[1,704,2048]{2,1,0:T(8,128)(2,1)}, u32[]{:S(2)}) copy-start(bf16[1,704,2048]{2,1,0:T(8,128)(2,1)} %param.29) | copy-start | bytes 8650756
  7.2 22.4 %copy-start.14 = (bf16[16,576]{1,0:T(8,128)(2,1)S(1)}, bf16[16,576]{1,0:T(8,128)(2,1)}, u32[]{:S(2)}) copy-start(bf16[16,576]{1,0:T(8,128)(2,1)} %param.17) | copy-start | bytes 55300
  7.2 83.3 %all-gather.2.cloned.1.call-start = ((), (), s32[]{:S(2)}) async-start(), calls=%async_computation.5 | async-start | bytes 2949120 | tf_op jit(solution)/shard_map/all_gather | solution.py:157
  7.3 24.1 %copy-start.16 = (s32[128]{0:T(128)}, s32[128]{0:T(128)S(1)}, u32[]{:S(2)}) copy-start(s32[128]{0:T(128)S(1)} %iota_add_fusion) | copy-start | bytes 1540
  8.3 23.1 %copy-start.18 = (s32[4,1]{0,1:T(1,128)}, s32[4,1]{0,1:T(1,128)S(1)}, u32[]{:S(2)}) copy-start(s32[4,1]{0,1:T(1,128)S(1)} %reduce-window.4) | copy-start | bytes 52
  9.0 22.4 %copy-start.17 = (s32[128]{0:T(128)}, s32[128]{0:T(128)S(1)}, u32[]{:S(2)}) copy-start(s32[128]{0:T(128)S(1)} %convert_reduce_fusion.1) | copy-start | bytes 1540
  31.4 48.6 %all-to-all-start = ((bf16[128,16,576]{2,1,0:T(8,128)(2,1)}), bf16[128,16,576]{2,1,0:T(8,128)(2,1)}, u32[]{:S(2)}, u32[]{:S(2)}) async-start(bf16[128,16,576]{2,1,0:T(8,128)(2,1)} %broadcast_in_dim.44), calls=%async_computation | async-start | bytes 5242880 | tf_op jit(solution)/shard_map/all_to_all | solution.py:105
  44.2 8.9 %copy-start.3 = (bf16[1,128,2048]{2,1,0:T(8,128)(2,1)S(1)}, bf16[1,128,2048]{2,1,0:T(8,128)(2,1)}, u32[]{:S(2)}) copy-start(bf16[1,128,2048]{2,1,0:T(8,128)(2,1)} %param.15) | copy-start | bytes 1572868
  53.1 5.6 %copy-start.13 = (f32[128,32]{0,1:T(8,128)S(1)}, f32[128,32]{0,1:T(8,128)}, u32[]{:S(2)}) copy-start(f32[128,32]{0,1:T(8,128)} %get-tuple-element.19) | copy-start | bytes 49156
  57.8 0.9 copy-start.7
  69.1 6.2 %copy-start.10 = (bf16[128,1024]{0,1:T(8,128)(2,1)S(1)}, bf16[128,1024]{0,1:T(8,128)(2,1)}, u32[]{:S(2)}) copy-start(bf16[128,1024]{0,1:T(8,128)(2,1)} %copy.66) | copy-start | bytes 786436
  90.5 6.6 %copy-start.2 = (f32[1024,2048]{1,0:T(8,128)S(1)}, f32[1024,2048]{1,0:T(8,128)}, u32[]{:S(2)}) copy-start(f32[1024,2048]{1,0:T(8,128)} %get-tuple-element.23) | copy-start | bytes 25165828
  103.3 1.7 copy-start.19
  105.0 2.6 copy-start.8
  105.0 3.5 copy-start.6
  107.5 2.5 copy-start.12
  110.0 0.8 copy-start.4
  114.1 13.6 %copy-start.5 = (bf16[128,2048]{1,0:T(8,128)(2,1)S(1)}, bf16[128,2048]{1,0:T(8,128)(2,1)}, u32[]{:S(2)}) copy-start(bf16[128,2048]{1,0:T(8,128)(2,1)} %copy-done.4) | copy-start | bytes 1572868
  114.1 65.9 %all-to-all-start.3 = ((bf16[128,1,8,2048]{3,2,1,0:T(8,128)(2,1)}), bf16[128,1,8,2048]{3,2,1,0:T(8,128)(2,1)}, u32[]{:S(2)}, u32[]{:S(2)}) async-start(bf16[128,1,8,2048]{3,2,1,0:T(8,128)(2,1)} %convert_bitcast_fusion.1), calls=%async_computation.3 | async-start | bytes 8388608 | tf_op jit(solution)/shard_map/all_to_all | solution.py:223
  180.0 58.4 %all-to-all-start.1 = ((bf16[128,1,8,2048]{3,2,1,0:T(8,128)(2,1)}), bf16[128,1,8,2048]{3,2,1,0:T(8,128)(2,1)}, u32[]{:S(2)}, u32[]{:S(2)}) async-start(bf16[128,1,8,2048]{3,2,1,0:T(8,128)(2,1)} %convert_bitcast_fusion.3), calls=%async_computation.1 | async-start | bytes 8388608 | tf_op jit(solution)/shard_map/all_to_all | solution.py:223
  238.4 57.9 %all-to-all-start.4 = ((bf16[128,1,8,2048]{3,2,1,0:T(8,128)(2,1)}), bf16[128,1,8,2048]{3,2,1,0:T(8,128)(2,1)}, u32[]{:S(2)}, u32[]{:S(2)}) async-start(bf16[128,1,8,2048]{3,2,1,0:T(8,128)(2,1)} %convert_bitcast_fusion), calls=%async_computation.4 | async-start | bytes 8388608 | tf_op jit(solution)/shard_map/all_to_all | solution.py:229
  259.7 42.7 %copy-start.15 = (f32[1,128,6]{1,0,2:T(1,128)S(1)}, f32[1,128,6]{1,0,2:T(1,128)}, u32[]{:S(2)}) copy-start(f32[1,128,6]{1,0,2:T(1,128)} %param.27) | copy-start | bytes 9220
  296.3 58.2 %all-to-all-start.2 = ((bf16[128,1,8,2048]{3,2,1,0:T(8,128)(2,1)}), bf16[128,1,8,2048]{3,2,1,0:T(8,128)(2,1)}, u32[]{:S(2)}, u32[]{:S(2)}) async-start(bf16[128,1,8,2048]{3,2,1,0:T(8,128)(2,1)} %convert_bitcast_fusion.2), calls=%async_computation.2 | async-start | bytes 8388608 | tf_op jit(solution)/shard_map/all_to_all | solution.py:229
  354.5 3.1 copy-start.11
  357.5 4.8 %copy-start.1 = (f32[64,8,2048]{2,1,0:T(8,128)S(1)}, f32[64,8,2048]{2,1,0:T(8,128)}, u32[]{:S(2)}) copy-start(f32[64,8,2048]{2,1,0:T(8,128)} %add_bitcast_fusion) | copy-start | bytes 12582916
  357.6 4.8 %copy-start.9 = (f32[128,64,8]{0,2,1:T(8,128)S(1)}, f32[128,64,8]{0,2,1:T(8,128)}, u32[]{:S(2)}) copy-start(f32[128,64,8]{0,2,1:T(8,128)} %get-tuple-element.9) | copy-start | bytes 786436
Sparse Core Ops, SparseCore 0:
  29.7 60.7 all-gather.1

commit v3 on v2

--- a/solution.py
+++ b/solution.py
@@ -49,9 +49,9 @@
     head_count = key_absorb.shape[0]
     plain_width = key_absorb.shape[1]
     latent_width = latent_gain.shape[0]
-    projected = jnp.dot(normed, query_weight, preferred_element_type=jnp.float32).reshape(
-        row_count, head_count, -1
-    )
+    projected = lax.optimization_barrier(
+        jnp.dot(normed, query_weight, preferred_element_type=jnp.float32)
+    ).reshape(row_count, head_count, -1)
     rope_width = projected.shape[-1] - plain_width
     cosine, sine_table = rope_tables(positions, rope_width)
     query_plain = projected[..., :plain_width].astype(jnp.bfloat16)

time: 378 us -> 378 us (level)
  local copies, waits for them, and re-layouts: 22.4 us -> 17.3 us
  waiting for transfers between devices: 174 us -> 179 us
    unnamed x43 -> x40, local copies, waits for them, and re-layouts: 11.7 us -> 4.2 us
    all_to_all x1, waiting for transfers between devices: 4.07 us -> 9.4 us  [gather_rows(): lax.all_to_all(copies, axes, split_axis=0, concat_axis=0, tiled=True)]
  transfers between devices with their start and end apart: 6 -> 6, of which waited for: 6 -> 6; matrix products, arithmetic and copies ran while one was open for 22% -> 21% of each run, Pallas kernels for 0% -> 0%
where the time goes in v3:
time: 378 us; the launch traced here: 374 us
  waiting for transfers between devices  179 us (47%)
  matrix products  82.4 us (22%)
  starting transfers between devices  44.1 us (12%)
  other arithmetic  22.6 us (6%)
  local copies, waits for them, and re-layouts  17.3 us (5%)
  between operations  14.6 us (4%)
  blocking collectives  14.1 us (4%)
    all_to_all x2, waiting for transfers between devices, on_device(): lax.all_to_all(outgoing, ('row', 'col', 'rep'), split_axis=0, concat_axis...  85.5 us
    all_to_all x2, waiting for transfers between devices, on_device(): lax.all_to_all(produced, ('row', 'col', 'rep'), split_axis=0, concat_axis...  82.5 us
    dot_general x2, matrix products, expert_apply(): joint = jnp.dot(rows, expert_gate_up[0], preferred_element_type=jnp.float32)  20.9 us
    all_to_all x2, starting transfers between devices, on_device(): lax.all_to_all(outgoing, ('row', 'col', 'rep'), split_axis=0, concat_axis...  19.7 us
    dot_general x2, matrix products, attend_block(): lax.dot_general(query_rows, key_block, (((1,), (1,)), ((), ())), preferre...  15.5 us
    all_gather x1, blocking collectives, on_device(): lax.all_gather(key_rows, 'col', axis=0, tiled=True)  14.1 us
    all_to_all x1, starting transfers between devices, gather_rows(): lax.all_to_all(copies, axes, split_axis=0, concat_axis=0, tiled=True)  12.8 us
    all_to_all x2, starting transfers between devices, on_device(): lax.all_to_all(produced, ('row', 'col', 'rep'), split_axis=0, concat_axis...  11.6 us
  transfers between devices with their start and end apart: 6, of which 6 were waited for; matrix products, arithmetic and copies ran while one was open for 21% of the time, Pallas kernels for 0%

profile of v3, /device:TPU:1, one launch (start us, length us, event | category | flops | bytes accessed | tf_op | source)
XLA Modules:
  0.0 374.3 jit_solution(14060971469454063496)
XLA Ops:
  11.0 2.7 fusion.81
  14.8 14.1 %all_gather.6 = bf16[512,576]{0,1:T(8,128)(2,1)} all-gather(bf16[128,576]{0,1:T(8,128)(2,1)S(1)} %pad_maximum_fusion.1), channel_id=1, replica_groups=mesh['row'=4,'col'=4,'rep'=8] {'col'}, dimensions={0}, use_global_device_ids=true | all-gather | bytes 737280 | tf_op jit(solution)/shard_map/all_gather | solution.py:158
  30.7 12.8 %all-to-all-start = ((bf16[128,16,576]{2,1,0:T(8,128)(2,1)}), bf16[128,16,576]{2,1,0:T(8,128)(2,1)}, u32[]{:S(2)}, u32[]{:S(2)}) async-start(bf16[128,16,576]{2,1,0:T(8,128)(2,1)} %broadcast_in_dim.44), calls=%async_computation | async-start | bytes 5242880 | tf_op jit(solution)/shard_map/all_to_all | solution.py:105
  45.0 4.7 %fusion.83 = f32[128,1536]{1,0:T(8,128)} fusion(bf16[2048,1536]{1,0:T(8,128)(2,1)} %param.19, bf16[1,128,2048]{2,1,0:T(8,128)(2,1)S(1)} %copy-done.3, f32[2048]{0:T(1024)S(1)} %convert_element_type.135, f32[128]{0:T(128)S(1)} %add_rsqrt_fusion.2), kind=kOutput, calls=%fused_computation.91 | convolution fusion | flops 806354944 | bytes 7610880 | tf_op jit(solution)/shard_map/dot_general | solution.py:53
  49.7 2.3 copy.81
  53.6 1.9 copy.106
  61.5 1.8 copy.95
  66.1 1.9 fusion.57
  69.9 9.4 %all-to-all-done = bf16[128,16,576]{2,1,0:T(8,128)(2,1)} async-done(((bf16[128,16,576]{2,1,0:T(8,128)(2,1)}), bf16[128,16,576]{2,1,0:T(8,128)(2,1)}, u32[]{:S(2)}, u32[]{:S(2)}) %all-to-all-start) | async-done | bytes 2359328 | tf_op jit(solution)/shard_map/all_to_all | solution.py:105
  79.3 8.9 %multiply_reduce_fusion = (f32[1024]{0:T(1024)S(1)}, f32[1024,2048]{1,0:T(8,128)}) fusion(bf16[2048,576]{1,0:T(8,128)(2,1)} %bitcast.9, bf16[128,8,576]{2,0,1:T(8,128)(2,1)} %pad_maximum_fusion), kind=kOutput, calls=%fused_computation.5 | convolution fusion | flops 2420112384 | bytes 11931648 | tf_op jit(solution)/shard_map/dot_general | solution.py:75
  90.0 6.5 %fusion.97 = (f32[1024]{0:T(1024)S(1)}, f32[1024,2048]{1,0:T(8,128)S(1)}) fusion(bf16[2048,576]{0,1:T(8,128)(2,1)} %all-gather.2.cloned.1.call-done, bf16[128,8,576]{2,0,1:T(8,128)(2,1)} %pad_maximum_fusion, s32[1024]{0:T(1024)} %ge.63, s32[2048]{0:T(1024)} %convert_reduce_fusion, s32[1024]{0:T(1024)} %eq.73), kind=kOutput, calls=%fused_computation.126 | convolution fusion | flops 2428500992 | bytes 11948032 | tf_op jit(solution)/shard_map/dot_general | solution.py:75
  96.6 2.1 fusion.3
  98.7 4.0 %fusion.9 = f32[1024,512]{1,0:T(8,128)S(1)} fusion(f32[1024,2048]{1,0:T(8,128)S(1)} %copy-done.2, f32[1024]{0:T(1024)S(1)} %get-tuple-element.19, bf16[2048,576]{1,0:T(8,128)(2,1)} %bitcast.9), kind=kOutput, calls=%fused_computation.14 | convolution fusion | flops 2153775104 | bytes 12587008 | tf_op jit(solution)/shard_map/dot_general | solution.py:85
  104.4 2.6 fusion.58
  110.3 3.3 convert_bitcast_fusion.1
  113.6 13.4 %all-to-all-start.3 = ((bf16[128,1,8,2048]{3,2,1,0:T(8,128)(2,1)}), bf16[128,1,8,2048]{3,2,1,0:T(8,128)(2,1)}, u32[]{:S(2)}, u32[]{:S(2)}) async-start(bf16[128,1,8,2048]{3,2,1,0:T(8,128)(2,1)} %convert_bitcast_fusion.1), calls=%async_computation.3 | async-start | bytes 8388608 | tf_op jit(solution)/shard_map/all_to_all | solution.py:223
  127.1 3.3 convert_bitcast_fusion.3
  130.4 49.0 %all-to-all-done.3 = bf16[128,1,8,2048]{3,2,1,0:T(8,128)(2,1)} async-done(((bf16[128,1,8,2048]{3,2,1,0:T(8,128)(2,1)}), bf16[128,1,8,2048]{3,2,1,0:T(8,128)(2,1)}, u32[]{:S(2)}, u32[]{:S(2)}) %all-to-all-start.3) | async-done | bytes 4194336 | tf_op jit(solution)/shard_map/all_to_all | solution.py:223
  179.4 6.2 %all-to-all-start.1 = ((bf16[128,1,8,2048]{3,2,1,0:T(8,128)(2,1)}), bf16[128,1,8,2048]{3,2,1,0:T(8,128)(2,1)}, u32[]{:S(2)}, u32[]{:S(2)}) async-start(bf16[128,1,8,2048]{3,2,1,0:T(8,128)(2,1)} %convert_bitcast_fusion.3), calls=%async_computation.1 | async-start | bytes 8388608 | tf_op jit(solution)/shard_map/all_to_all | solution.py:223
  185.6 10.4 %fusion.5 = f32[1024,1408]{1,0:T(8,128)S(1)} fusion(bf16[1,2048,1408]{2,1,0:T(8,128)(2,1)} %param.28, bf16[128,1,8,2048]{3,2,1,0:T(8,128)(2,1)} %all-to-all-done.3), kind=kOutput, calls=%fused_computation.10 | convolution fusion | flops 5905580032 | bytes 15728640 | tf_op jit(solution)/shard_map/dot_general | solution.py:96
  196.1 5.2 %convert_bitcast_fusion = bf16[128,1,8,2048]{3,2,1,0:T(8,128)(2,1)} fusion(bf16[1,704,2048]{2,1,0:T(8,128)(2,1)S(1)} %copy-done, f32[1024,1408]{1,0:T(8,128)S(1)} %fusion.5), kind=kOutput, calls=%fused_computation.23 | convolution fusion | flops 2959212544 | bytes 13369344 | tf_op jit(solution)/shard_map/dot_general | solution.py:98
  201.2 36.5 %all-to-all-done.1 = bf16[128,1,8,2048]{3,2,1,0:T(8,128)(2,1)} async-done(((bf16[128,1,8,2048]{3,2,1,0:T(8,128)(2,1)}), bf16[128,1,8,2048]{3,2,1,0:T(8,128)(2,1)}, u32[]{:S(2)}, u32[]{:S(2)}) %all-to-all-start.1) | async-done | bytes 4194336 | tf_op jit(solution)/shard_map/all_to_all | solution.py:223
  237.7 5.6 %all-to-all-start.4 = ((bf16[128,1,8,2048]{3,2,1,0:T(8,128)(2,1)}), bf16[128,1,8,2048]{3,2,1,0:T(8,128)(2,1)}, u32[]{:S(2)}, u32[]{:S(2)}) async-start(bf16[128,1,8,2048]{3,2,1,0:T(8,128)(2,1)} %convert_bitcast_fusion), calls=%async_computation.4 | async-start | bytes 8388608 | tf_op jit(solution)/shard_map/all_to_all | solution.py:229
  243.3 10.4 %fusion.7 = f32[1024,1408]{1,0:T(8,128)S(1)} fusion(bf16[1,2048,1408]{2,1,0:T(8,128)(2,1)} %param.28, bf16[128,1,8,2048]{3,2,1,0:T(8,128)(2,1)} %all-to-all-done.1), kind=kOutput, calls=%fused_computation.12 | convolution fusion | flops 5905580032 | bytes 15728640 | tf_op jit(solution)/shard_map/dot_general | solution.py:96
  253.8 5.2 %convert_bitcast_fusion.2 = bf16[128,1,8,2048]{3,2,1,0:T(8,128)(2,1)} fusion(bf16[1,704,2048]{2,1,0:T(8,128)(2,1)S(1)} %copy-done, f32[1024,1408]{1,0:T(8,128)S(1)} %fusion.7), kind=kOutput, calls=%fused_computation.26 | convolution fusion | flops 2959212544 | bytes 13369344 | tf_op jit(solution)/shard_map/dot_general | solution.py:98
  259.0 36.6 %all-to-all-done.4 = bf16[128,1,8,2048]{3,2,1,0:T(8,128)(2,1)} async-done(((bf16[128,1,8,2048]{3,2,1,0:T(8,128)(2,1)}), bf16[128,1,8,2048]{3,2,1,0:T(8,128)(2,1)}, u32[]{:S(2)}, u32[]{:S(2)}) %all-to-all-start.4) | async-done | bytes 4194336 | tf_op jit(solution)/shard_map/all_to_all | solution.py:229
  295.7 6.0 %all-to-all-start.2 = ((bf16[128,1,8,2048]{3,2,1,0:T(8,128)(2,1)}), bf16[128,1,8,2048]{3,2,1,0:T(8,128)(2,1)}, u32[]{:S(2)}, u32[]{:S(2)}) async-start(bf16[128,1,8,2048]{3,2,1,0:T(8,128)(2,1)} %convert_bitcast_fusion.2), calls=%async_computation.2 | async-start | bytes 8388608 | tf_op jit(solution)/shard_map/all_to_all | solution.py:229
  303.0 5.0 %add_bitcast_fusion = f32[64,8,2048]{2,1,0:T(8,128)} fusion(bf16[64,2,8,2048]{3,2,1,0:T(8,128)(2,1)} %bitcast.33), kind=kLoop, calls=%fused_computation.22 | loop fusion | flops 3145728 | bytes 8388608 | tf_op jit(solution)/shard_map/add | solution.py:232
  308.0 45.8 %all-to-all-done.2 = bf16[128,1,8,2048]{3,2,1,0:T(8,128)(2,1)} async-done(((bf16[128,1,8,2048]{3,2,1,0:T(8,128)(2,1)}), bf16[128,1,8,2048]{3,2,1,0:T(8,128)(2,1)}, u32[]{:S(2)}, u32[]{:S(2)}) %all-to-all-start.2) | async-done | bytes 4194336 | tf_op jit(solution)/shard_map/all_to_all | solution.py:229
  353.8 3.1 add_bitcast_fusion.1
  356.9 4.7 %fusion.27 = f32[128,2048]{1,0:T(8,128)S(1)} fusion(f32[64,8,2048]{2,1,0:T(8,128)S(1)} %add_bitcast_fusion.1, f32[128,64,8]{0,2,1:T(8,128)S(1)} %copy-done.10), kind=kOutput, calls=%fused_computation.41 | convolution fusion | flops 1610612736 | bytes 5505024 | tf_op jit(solution)/shard_map/dot_general | solution.py:233
  361.7 5.6 %fusion.43 = bf16[1,128,2048]{2,1,0:T(8,128)(2,1)} fusion(f32[128,2048]{1,0:T(8,128)S(1)} %fusion.27, f32[64,8,2048]{2,1,0:T(8,128)S(1)} %copy-done.1, bf16[128,2048]{1,0:T(8,128)(2,1)S(1)} %copy-done.5, f32[128,64,8]{0,2,1:T(8,128)S(1)} %copy-done.9), kind=kOutput, calls=%fused_computation.48 | convolution fusion | flops 1611661312 | bytes 6553600 | tf_op jit(solution)/shard_map/dot_general | solution.py:233
  (89 shorter events, 28.3 us)
Async XLA Ops:
  7.2 188.9 %copy-start = (bf16[1,704,2048]{2,1,0:T(8,128)(2,1)S(1)}, bf16[1,704,2048]{2,1,0:T(8,128)(2,1)}, u32[]{:S(2)}) copy-start(bf16[1,704,2048]{2,1,0:T(8,128)(2,1)} %param.29) | copy-start | bytes 8650756
  7.2 21.8 %copy-start.12 = (bf16[16,576]{1,0:T(8,128)(2,1)S(1)}, bf16[16,576]{1,0:T(8,128)(2,1)}, u32[]{:S(2)}) copy-start(bf16[16,576]{1,0:T(8,128)(2,1)} %param.17) | copy-start | bytes 55300
  7.2 82.8 %all-gather.2.cloned.1.call-start = ((), (), s32[]{:S(2)}) async-start(), calls=%async_computation.5 | async-start | bytes 2949120 | tf_op jit(solution)/shard_map/all_gather | solution.py:157
  8.2 1.5 copy-start.16
  28.9 16.0 %copy-start.3 = (bf16[1,128,2048]{2,1,0:T(8,128)(2,1)S(1)}, bf16[1,128,2048]{2,1,0:T(8,128)(2,1)}, u32[]{:S(2)}) copy-start(bf16[1,128,2048]{2,1,0:T(8,128)(2,1)} %param.15) | copy-start | bytes 1572868
  30.7 48.6 %all-to-all-start = ((bf16[128,16,576]{2,1,0:T(8,128)(2,1)}), bf16[128,16,576]{2,1,0:T(8,128)(2,1)}, u32[]{:S(2)}, u32[]{:S(2)}) async-start(bf16[128,16,576]{2,1,0:T(8,128)(2,1)} %broadcast_in_dim.44), calls=%async_computation | async-start | bytes 5242880 | tf_op jit(solution)/shard_map/all_to_all | solution.py:105
  45.0 13.1 %copy-start.14 = (s32[1,128,6]{1,0,2:T(1,128)S(1)}, s32[1,128,6]{1,0,2:T(1,128)}, u32[]{:S(2)}) copy-start(s32[1,128,6]{1,0,2:T(1,128)} %param.26) | copy-start | bytes 9220
  49.7 13.7 %copy-start.13 = (bf16[2048]{0:T(1024)(128)(2,1)S(1)}, bf16[2048]{0:T(1024)(128)(2,1)}, u32[]{:S(2)}) copy-start(bf16[2048]{0:T(1024)(128)(2,1)} %param.25) | copy-start | bytes 12292
  63.3 5.9 %copy-start.8 = (bf16[128,1024]{0,1:T(8,128)(2,1)S(1)}, bf16[128,1024]{0,1:T(8,128)(2,1)}, u32[]{:S(2)}) copy-start(bf16[128,1024]{0,1:T(8,128)(2,1)} %copy.95) | copy-start | bytes 786436
  90.0 6.6 %copy-start.2 = (f32[1024,2048]{1,0:T(8,128)S(1)}, f32[1024,2048]{1,0:T(8,128)}, u32[]{:S(2)}) copy-start(f32[1024,2048]{1,0:T(8,128)} %get-tuple-element.25) | copy-start | bytes 25165828
  102.8 1.7 copy-start.17
  104.4 2.6 copy-start.7
  104.4 3.5 copy-start.6
  107.0 2.5 copy-start.11
  109.5 0.8 copy-start.4
  113.6 13.5 %copy-start.5 = (bf16[128,2048]{1,0:T(8,128)(2,1)S(1)}, bf16[128,2048]{1,0:T(8,128)(2,1)}, u32[]{:S(2)}) copy-start(bf16[128,2048]{1,0:T(8,128)(2,1)} %copy-done.4) | copy-start | bytes 1572868
  113.6 65.7 %all-to-all-start.3 = ((bf16[128,1,8,2048]{3,2,1,0:T(8,128)(2,1)}), bf16[128,1,8,2048]{3,2,1,0:T(8,128)(2,1)}, u32[]{:S(2)}, u32[]{:S(2)}) async-start(bf16[128,1,8,2048]{3,2,1,0:T(8,128)(2,1)} %convert_bitcast_fusion.1), calls=%async_computation.3 | async-start | bytes 8388608 | tf_op jit(solution)/shard_map/all_to_all | solution.py:223
  179.4 58.4 %all-to-all-start.1 = ((bf16[128,1,8,2048]{3,2,1,0:T(8,128)(2,1)}), bf16[128,1,8,2048]{3,2,1,0:T(8,128)(2,1)}, u32[]{:S(2)}, u32[]{:S(2)}) async-start(bf16[128,1,8,2048]{3,2,1,0:T(8,128)(2,1)} %convert_bitcast_fusion.3), calls=%async_computation.1 | async-start | bytes 8388608 | tf_op jit(solution)/shard_map/all_to_all | solution.py:223
  237.7 57.9 %all-to-all-start.4 = ((bf16[128,1,8,2048]{3,2,1,0:T(8,128)(2,1)}), bf16[128,1,8,2048]{3,2,1,0:T(8,128)(2,1)}, u32[]{:S(2)}, u32[]{:S(2)}) async-start(bf16[128,1,8,2048]{3,2,1,0:T(8,128)(2,1)} %convert_bitcast_fusion), calls=%async_computation.4 | async-start | bytes 8388608 | tf_op jit(solution)/shard_map/all_to_all | solution.py:229
  259.0 42.7 %copy-start.15 = (f32[1,128,6]{1,0,2:T(1,128)S(1)}, f32[1,128,6]{1,0,2:T(1,128)}, u32[]{:S(2)}) copy-start(f32[1,128,6]{1,0,2:T(1,128)} %param.27) | copy-start | bytes 9220
  295.7 58.2 %all-to-all-start.2 = ((bf16[128,1,8,2048]{3,2,1,0:T(8,128)(2,1)}), bf16[128,1,8,2048]{3,2,1,0:T(8,128)(2,1)}, u32[]{:S(2)}, u32[]{:S(2)}) async-start(bf16[128,1,8,2048]{3,2,1,0:T(8,128)(2,1)} %convert_bitcast_fusion.2), calls=%async_computation.2 | async-start | bytes 8388608 | tf_op jit(solution)/shard_map/all_to_all | solution.py:229
  353.8 3.1 copy-start.10
  356.9 4.8 %copy-start.1 = (f32[64,8,2048]{2,1,0:T(8,128)S(1)}, f32[64,8,2048]{2,1,0:T(8,128)}, u32[]{:S(2)}) copy-start(f32[64,8,2048]{2,1,0:T(8,128)} %add_bitcast_fusion) | copy-start | bytes 12582916
  356.9 4.8 %copy-start.9 = (f32[128,64,8]{0,2,1:T(8,128)S(1)}, f32[128,64,8]{0,2,1:T(8,128)}, u32[]{:S(2)}) copy-start(f32[128,64,8]{0,2,1:T(8,128)} %get-tuple-element.11) | copy-start | bytes 786436
Sparse Core Ops, SparseCore 0:
  29.1 60.8 all-gather.1

commit v4 on v3

--- a/solution.py
+++ b/solution.py
@@ -201,7 +201,7 @@
     pick_slots = pick_table.reshape(token_count, top_count, E, CAP)
     device_count = lax.axis_size(("row", "col", "rep"))
     per_device = expert_gate_up.shape[0]
-    chunk_count = 2
+    chunk_count = 4
     chunk = CAP // chunk_count
     gate_table = jnp.sum(
         pick_slots.astype(jnp.float32) * gate_weights[0][:, :, None, None], axis=1

time: 378 us -> 432 us (1.14)
  local copies, waits for them, and re-layouts: 17.3 us -> 65.7 us
  waiting for transfers between devices: 179 us -> 152 us
  starting transfers between devices: 44.1 us -> 62.4 us
  matrix products: 82.4 us -> 91.6 us
  other arithmetic: 22.6 us -> 27.5 us
    reshape x0 -> x12, local copies, waits for them, and re-layouts: none -> 48.7 us  [the longest x4 16.4 us: expert_apply(): return produced.astype(jnp.bfloat16).reshape(token_rows.shape)]
    all_to_all x2 -> x4, waiting for transfers between devices: 82.5 us -> 55.6 us  [on_device(): lax.all_to_all(produced, ('row', 'col', 'rep'), split_axis=0, concat_axis...]
    all_to_all x2 -> x4, starting transfers between devices: 19.7 us -> 28.7 us  [on_device(): lax.all_to_all(outgoing, ('row', 'col', 'rep'), split_axis=0, concat_axis...]
    all_to_all x2 -> x4, starting transfers between devices: 11.6 us -> 20.6 us  [on_device(): lax.all_to_all(produced, ('row', 'col', 'rep'), split_axis=0, concat_axis...]
    add x2 -> x4, other arithmetic: 8.06 us -> 13.8 us  [on_device(): returned[:, 0].astype(jnp.float32) + returned[:, 1].astype(jnp.float32)]
    dot_general x2 -> x4, matrix products: 20.9 us -> 25.5 us  [expert_apply(): joint = jnp.dot(rows, expert_gate_up[0], preferred_element_type=jnp.float32)]
    dot_general x2 -> x4, matrix products: 10.4 us -> 12.9 us  [expert_apply(): jnp.dot(active, expert_down[0], preferred_element_type=jnp.float32)]
    all_to_all x2 -> x4, waiting for transfers between devices: 85.5 us -> 83.9 us  [on_device(): lax.all_to_all(outgoing, ('row', 'col', 'rep'), split_axis=0, concat_axis...]
  transfers between devices with their start and end apart: 6 -> 10, of which waited for: 6 -> 10; matrix products, arithmetic and copies ran while one was open for 21% -> 32% of each run, Pallas kernels for 0% -> 0%
where the time goes in v4:
time: 432 us; the launch traced here: 428 us
  waiting for transfers between devices  152 us (35%)
  matrix products  91.6 us (21%)
  local copies, waits for them, and re-layouts  65.7 us (15%)
  starting transfers between devices  62.4 us (14%)
  other arithmetic  27.5 us (6%)
  between operations  14.8 us (3%)
  blocking collectives  14.1 us (3%)
    all_to_all x4, waiting for transfers between devices, on_device(): lax.all_to_all(outgoing, ('row', 'col', 'rep'), split_axis=0, concat_axis...  83.9 us
    all_to_all x4, waiting for transfers between devices, on_device(): lax.all_to_all(produced, ('row', 'col', 'rep'), split_axis=0, concat_axis...  55.6 us
    all_to_all x4, starting transfers between devices, on_device(): lax.all_to_all(outgoing, ('row', 'col', 'rep'), split_axis=0, concat_axis...  28.7 us
    dot_general x4, matrix products, expert_apply(): joint = jnp.dot(rows, expert_gate_up[0], preferred_element_type=jnp.float32)  25.5 us
    all_to_all x4, starting transfers between devices, on_device(): lax.all_to_all(produced, ('row', 'col', 'rep'), split_axis=0, concat_axis...  20.6 us
    reshape x4, local copies, waits for them, and re-layouts, expert_apply(): return produced.astype(jnp.bfloat16).reshape(token_rows.shape)  16.4 us
    reshape x4, local copies, waits for them, and re-layouts, on_device(): outgoing = jnp.einsum('tj,td->jd', send_table[..., window].reshape(token_...  16.4 us
    reshape x4, local copies, waits for them, and re-layouts, expert_apply(): rows = token_rows.reshape(-1, token_rows.shape[-1])  15.9 us
  transfers between devices with their start and end apart: 10, of which 10 were waited for; matrix products, arithmetic and copies ran while one was open for 32% of the time, Pallas kernels for 0%

profile of v4, /device:TPU:1, one launch (start us, length us, event | category | flops | bytes accessed | tf_op | source)
XLA Modules:
  0.0 427.6 jit_solution(15698038112837365897)
XLA Ops:
  14.2 14.1 %all_gather.6 = bf16[512,576]{0,1:T(8,128)(2,1)} all-gather(bf16[128,576]{0,1:T(8,128)(2,1)S(1)} %pad_maximum_fusion.1), channel_id=1, replica_groups=mesh['row'=4,'col'=4,'rep'=8] {'col'}, dimensions={0}, use_global_device_ids=true | all-gather | bytes 737280 | tf_op jit(solution)/shard_map/all_gather | solution.py:158
  30.0 13.1 %all-to-all-start = ((bf16[128,16,576]{2,1,0:T(8,128)(2,1)}), bf16[128,16,576]{2,1,0:T(8,128)(2,1)}, u32[]{:S(2)}, u32[]{:S(2)}) async-start(bf16[128,16,576]{2,1,0:T(8,128)(2,1)} %broadcast_in_dim.48), calls=%async_computation | async-start | bytes 5242880 | tf_op jit(solution)/shard_map/all_to_all | solution.py:105
  44.6 4.7 %fusion.79 = f32[128,1536]{1,0:T(8,128)} fusion(bf16[2048,1536]{1,0:T(8,128)(2,1)} %param.19, bf16[1,128,2048]{2,1,0:T(8,128)(2,1)S(1)} %copy-done.3, f32[2048]{0:T(1024)S(1)} %convert_element_type.169, f32[128]{0:T(128)S(1)} %add_rsqrt_fusion.2), kind=kOutput, calls=%fused_computation.109 | convolution fusion | flops 806354944 | bytes 7610880 | tf_op jit(solution)/shard_map/dot_general | solution.py:53
  68.4 10.5 %all-to-all-done = bf16[128,16,576]{2,1,0:T(8,128)(2,1)} async-done(((bf16[128,16,576]{2,1,0:T(8,128)(2,1)}), bf16[128,16,576]{2,1,0:T(8,128)(2,1)}, u32[]{:S(2)}, u32[]{:S(2)}) %all-to-all-start) | async-done | bytes 2359328 | tf_op jit(solution)/shard_map/all_to_all | solution.py:105
  79.0 9.0 %multiply_reduce_fusion = (f32[1024]{0:T(1024)S(1)}, f32[1024,2048]{1,0:T(8,128)}) fusion(bf16[2048,576]{1,0:T(8,128)(2,1)} %bitcast.9, bf16[128,8,576]{2,0,1:T(8,128)(2,1)} %pad_maximum_fusion), kind=kOutput, calls=%fused_computation.5 | convolution fusion | flops 2420112384 | bytes 11931648 | tf_op jit(solution)/shard_map/dot_general | solution.py:75
  89.4 6.6 %fusion.101 = (f32[1024]{0:T(1024)S(1)}, f32[1024,2048]{1,0:T(8,128)S(1)}) fusion(bf16[2048,576]{0,1:T(8,128)(2,1)} %all-gather.2.cloned.1.call-done, bf16[128,8,576]{2,0,1:T(8,128)(2,1)} %pad_maximum_fusion, s32[1024]{0:T(1024)S(1)} %copy-done.19, s32[2048]{0:T(1024)S(1)} %copy-done.16, s32[1024]{0:T(1024)S(1)} %copy-done.18), kind=kOutput, calls=%fused_computation.150 | convolution fusion | flops 2428500992 | bytes 11948032 | tf_op jit(solution)/shard_map/dot_general | solution.py:75
  111.2 4.1 reshape.292
  115.3 13.7 %all-to-all-start.3 = ((bf16[128,1,4,2048]{3,2,1,0:T(4,128)(2,1)}), bf16[128,1,4,2048]{3,2,1,0:T(4,128)(2,1)}, u32[]{:S(2)}, u32[]{:S(2)}) async-start(bf16[128,1,4,2048]{3,2,1,0:T(4,128)(2,1)} %bitcast.129), calls=%async_computation.3 | async-start | bytes 4194304 | tf_op jit(solution)/shard_map/all_to_all | solution.py:223
  132.1 4.1 reshape.287
  136.2 23.1 %all-to-all-done.3 = bf16[128,1,4,2048]{3,2,1,0:T(4,128)(2,1)} async-done(((bf16[128,1,4,2048]{3,2,1,0:T(4,128)(2,1)}), bf16[128,1,4,2048]{3,2,1,0:T(4,128)(2,1)}, u32[]{:S(2)}, u32[]{:S(2)}) %all-to-all-start.3) | async-done | bytes 2097184 | tf_op jit(solution)/shard_map/all_to_all | solution.py:223
  159.3 4.9 %all-to-all-start.1 = ((bf16[128,1,4,2048]{3,2,1,0:T(4,128)(2,1)}), bf16[128,1,4,2048]{3,2,1,0:T(4,128)(2,1)}, u32[]{:S(2)}, u32[]{:S(2)}) async-start(bf16[128,1,4,2048]{3,2,1,0:T(4,128)(2,1)} %bitcast.128), calls=%async_computation.1 | async-start | bytes 4194304 | tf_op jit(solution)/shard_map/all_to_all | solution.py:223
  170.5 24.1 %all-to-all-done.1 = bf16[128,1,4,2048]{3,2,1,0:T(4,128)(2,1)} async-done(((bf16[128,1,4,2048]{3,2,1,0:T(4,128)(2,1)}), bf16[128,1,4,2048]{3,2,1,0:T(4,128)(2,1)}, u32[]{:S(2)}, u32[]{:S(2)}) %all-to-all-start.1) | async-done | bytes 2097184 | tf_op jit(solution)/shard_map/all_to_all | solution.py:223
  194.6 5.1 %all-to-all-start.5 = ((bf16[128,1,4,2048]{3,2,1,0:T(4,128)(2,1)}), bf16[128,1,4,2048]{3,2,1,0:T(4,128)(2,1)}, u32[]{:S(2)}, u32[]{:S(2)}) async-start(bf16[128,1,4,2048]{3,2,1,0:T(4,128)(2,1)} %bitcast.123), calls=%async_computation.5 | async-start | bytes 4194304 | tf_op jit(solution)/shard_map/all_to_all | solution.py:223
  201.9 4.1 reshape.302
  206.0 24.1 %all-to-all-done.5 = bf16[128,1,4,2048]{3,2,1,0:T(4,128)(2,1)} async-done(((bf16[128,1,4,2048]{3,2,1,0:T(4,128)(2,1)}), bf16[128,1,4,2048]{3,2,1,0:T(4,128)(2,1)}, u32[]{:S(2)}, u32[]{:S(2)}) %all-to-all-start.5) | async-done | bytes 2097184 | tf_op jit(solution)/shard_map/all_to_all | solution.py:223
  230.1 4.9 %all-to-all-start.7 = ((bf16[128,1,4,2048]{3,2,1,0:T(4,128)(2,1)}), bf16[128,1,4,2048]{3,2,1,0:T(4,128)(2,1)}, u32[]{:S(2)}, u32[]{:S(2)}) async-start(bf16[128,1,4,2048]{3,2,1,0:T(4,128)(2,1)} %bitcast.125), calls=%async_computation.7 | async-start | bytes 4194304 | tf_op jit(solution)/shard_map/all_to_all | solution.py:223
  239.0 6.4 %fusion.9 = f32[512,1408]{1,0:T(8,128)S(1)} fusion(bf16[512,2048]{1,0:T(8,128)(2,1)} %reshape.293, bf16[1,2048,1408]{2,1,0:T(8,128)(2,1)} %param.28), kind=kOutput, calls=%fused_computation.14 | convolution fusion | flops 2952790016 | bytes 10747904 | tf_op jit(solution)/shard_map/dot_general | solution.py:96
  248.6 4.1 reshape.294
  252.7 12.7 %all-to-all-done.7 = bf16[128,1,4,2048]{3,2,1,0:T(4,128)(2,1)} async-done(((bf16[128,1,4,2048]{3,2,1,0:T(4,128)(2,1)}), bf16[128,1,4,2048]{3,2,1,0:T(4,128)(2,1)}, u32[]{:S(2)}, u32[]{:S(2)}) %all-to-all-start.7) | async-done | bytes 2097184 | tf_op jit(solution)/shard_map/all_to_all | solution.py:223
  265.4 4.9 %all-to-all-start.4 = ((bf16[128,1,4,2048]{3,2,1,0:T(4,128)(2,1)}), bf16[128,1,4,2048]{3,2,1,0:T(4,128)(2,1)}, u32[]{:S(2)}, u32[]{:S(2)}) async-start(bf16[128,1,4,2048]{3,2,1,0:T(4,128)(2,1)} %bitcast.126), calls=%async_computation.4 | async-start | bytes 4194304 | tf_op jit(solution)/shard_map/all_to_all | solution.py:229
  274.3 6.4 %fusion.11 = f32[512,1408]{1,0:T(8,128)S(1)} fusion(bf16[512,2048]{1,0:T(8,128)(2,1)} %reshape.288, bf16[1,2048,1408]{2,1,0:T(8,128)(2,1)} %param.28), kind=kOutput, calls=%fused_computation.16 | convolution fusion | flops 2952790016 | bytes 10747904 | tf_op jit(solution)/shard_map/dot_general | solution.py:96
  283.9 4.1 reshape.289
  288.0 12.7 %all-to-all-done.4 = bf16[128,1,4,2048]{3,2,1,0:T(4,128)(2,1)} async-done(((bf16[128,1,4,2048]{3,2,1,0:T(4,128)(2,1)}), bf16[128,1,4,2048]{3,2,1,0:T(4,128)(2,1)}, u32[]{:S(2)}, u32[]{:S(2)}) %all-to-all-start.4) | async-done | bytes 2097184 | tf_op jit(solution)/shard_map/all_to_all | solution.py:229
  300.7 5.5 %all-to-all-start.2 = ((bf16[128,1,4,2048]{3,2,1,0:T(4,128)(2,1)}), bf16[128,1,4,2048]{3,2,1,0:T(4,128)(2,1)}, u32[]{:S(2)}, u32[]{:S(2)}) async-start(bf16[128,1,4,2048]{3,2,1,0:T(4,128)(2,1)} %bitcast.127), calls=%async_computation.2 | async-start | bytes 4194304 | tf_op jit(solution)/shard_map/all_to_all | solution.py:229
  310.2 6.4 %fusion.7 = f32[512,1408]{1,0:T(8,128)S(1)} fusion(bf16[512,2048]{1,0:T(8,128)(2,1)} %reshape.298, bf16[1,2048,1408]{2,1,0:T(8,128)(2,1)} %param.28), kind=kOutput, calls=%fused_computation.12 | convolution fusion | flops 2952790016 | bytes 10747904 | tf_op jit(solution)/shard_map/dot_general | solution.py:96
  319.8 4.1 reshape.299
  323.9 12.5 %all-to-all-done.2 = bf16[128,1,4,2048]{3,2,1,0:T(4,128)(2,1)} async-done(((bf16[128,1,4,2048]{3,2,1,0:T(4,128)(2,1)}), bf16[128,1,4,2048]{3,2,1,0:T(4,128)(2,1)}, u32[]{:S(2)}, u32[]{:S(2)}) %all-to-all-start.2) | async-done | bytes 2097184 | tf_op jit(solution)/shard_map/all_to_all | solution.py:229
  336.5 5.1 %all-to-all-start.6 = ((bf16[128,1,4,2048]{3,2,1,0:T(4,128)(2,1)}), bf16[128,1,4,2048]{3,2,1,0:T(4,128)(2,1)}, u32[]{:S(2)}, u32[]{:S(2)}) async-start(bf16[128,1,4,2048]{3,2,1,0:T(4,128)(2,1)} %bitcast.124), calls=%async_computation.6 | async-start | bytes 4194304 | tf_op jit(solution)/shard_map/all_to_all | solution.py:229
  345.5 6.4 %fusion.5 = f32[512,1408]{1,0:T(8,128)S(1)} fusion(bf16[512,2048]{1,0:T(8,128)(2,1)} %reshape.303, bf16[1,2048,1408]{2,1,0:T(8,128)(2,1)} %param.28), kind=kOutput, calls=%fused_computation.10 | convolution fusion | flops 2952790016 | bytes 10747904 | tf_op jit(solution)/shard_map/dot_general | solution.py:96
  359.2 12.7 %all-to-all-done.6 = bf16[128,1,4,2048]{3,2,1,0:T(4,128)(2,1)} async-done(((bf16[128,1,4,2048]{3,2,1,0:T(4,128)(2,1)}), bf16[128,1,4,2048]{3,2,1,0:T(4,128)(2,1)}, u32[]{:S(2)}, u32[]{:S(2)}) %all-to-all-start.6) | async-done | bytes 2097184 | tf_op jit(solution)/shard_map/all_to_all | solution.py:229
  371.9 5.1 %all-to-all-start.8 = ((bf16[128,1,4,2048]{3,2,1,0:T(4,128)(2,1)}), bf16[128,1,4,2048]{3,2,1,0:T(4,128)(2,1)}, u32[]{:S(2)}, u32[]{:S(2)}) async-start(bf16[128,1,4,2048]{3,2,1,0:T(4,128)(2,1)} %bitcast.122), calls=%async_computation.8 | async-start | bytes 4194304 | tf_op jit(solution)/shard_map/all_to_all | solution.py:229
  389.5 17.7 %all-to-all-done.8 = bf16[128,1,4,2048]{3,2,1,0:T(4,128)(2,1)} async-done(((bf16[128,1,4,2048]{3,2,1,0:T(4,128)(2,1)}), bf16[128,1,4,2048]{3,2,1,0:T(4,128)(2,1)}, u32[]{:S(2)}, u32[]{:S(2)}) %all-to-all-start.8) | async-done | bytes 2097184 | tf_op jit(solution)/shard_map/all_to_all | solution.py:229
  (135 shorter events, 115.9 us)
Async XLA Ops:
  7.2 238.2 %copy-start = (bf16[1,704,2048]{2,1,0:T(8,128)(2,1)S(1)}, bf16[1,704,2048]{2,1,0:T(8,128)(2,1)}, u32[]{:S(2)}) copy-start(bf16[1,704,2048]{2,1,0:T(8,128)(2,1)} %param.29) | copy-start | bytes 8650756
  7.2 6.6 %copy-start.22 = (bf16[512]{0:T(512)(128)(2,1)S(1)}, bf16[512]{0:T(512)(128)(2,1)}, u32[]{:S(2)}) copy-start(bf16[512]{0:T(512)(128)(2,1)} %param.21) | copy-start | bytes 3076
  7.2 82.2 %all-gather.2.cloned.1.call-start = ((), (), s32[]{:S(2)}) async-start(), calls=%async_computation.9 | async-start | bytes 2949120 | tf_op jit(solution)/shard_map/all_gather | solution.py:157
  11.0 17.3 %copy-start.15 = (bf16[16,576]{1,0:T(8,128)(2,1)S(1)}, bf16[16,576]{1,0:T(8,128)(2,1)}, u32[]{:S(2)}) copy-start(bf16[16,576]{1,0:T(8,128)(2,1)} %param.17) | copy-start | bytes 55300
  30.0 14.6 %copy-start.3 = (bf16[1,128,2048]{2,1,0:T(8,128)(2,1)S(1)}, bf16[1,128,2048]{2,1,0:T(8,128)(2,1)}, u32[]{:S(2)}) copy-start(bf16[1,128,2048]{2,1,0:T(8,128)(2,1)} %param.15) | copy-start | bytes 1572868
  30.0 48.9 %all-to-all-start = ((bf16[128,16,576]{2,1,0:T(8,128)(2,1)}), bf16[128,16,576]{2,1,0:T(8,128)(2,1)}, u32[]{:S(2)}, u32[]{:S(2)}) async-start(bf16[128,16,576]{2,1,0:T(8,128)(2,1)} %broadcast_in_dim.48), calls=%async_computation | async-start | bytes 5242880 | tf_op jit(solution)/shard_map/all_to_all | solution.py:105
  49.3 7.6 %copy-start.20 = (s32[1,128,6]{1,0,2:T(1,128)S(1)}, s32[1,128,6]{1,0,2:T(1,128)}, u32[]{:S(2)}) copy-start(s32[1,128,6]{1,0,2:T(1,128)} %param.26) | copy-start | bytes 9220
  51.6 10.6 %copy-start.17 = (bf16[2048]{0:T(1024)(128)(2,1)S(1)}, bf16[2048]{0:T(1024)(128)(2,1)}, u32[]{:S(2)}) copy-start(bf16[2048]{0:T(1024)(128)(2,1)} %param.25) | copy-start | bytes 12292
  62.2 2.7 copy-start.8
  78.9 10.4 %copy-start.16 = (s32[2048]{0:T(1024)S(1)}, s32[2048]{0:T(1024)}, u32[]{:S(2)}) copy-start(s32[2048]{0:T(1024)} %convert_reduce_fusion) | copy-start | bytes 24580
  78.9 10.4 %copy-start.18 = (s32[1024]{0:T(1024)S(1)}, s32[1024]{0:T(1024)}, u32[]{:S(2)}) copy-start(s32[1024]{0:T(1024)} %eq.73) | copy-start | bytes 12292
  79.0 10.4 %copy-start.19 = (s32[1024]{0:T(1024)S(1)}, s32[1024]{0:T(1024)}, u32[]{:S(2)}) copy-start(s32[1024]{0:T(1024)} %ge.63) | copy-start | bytes 12292
  89.4 6.6 %copy-start.2 = (f32[1024,2048]{1,0:T(8,128)S(1)}, f32[1024,2048]{1,0:T(8,128)}, u32[]{:S(2)}) copy-start(f32[1024,2048]{1,0:T(8,128)} %get-tuple-element.29) | copy-start | bytes 25165828
  102.1 1.7 copy-start.24
  103.8 2.6 copy-start.9
  103.8 3.5 copy-start.7
  107.5 1.6 copy-start.14
  115.3 43.9 %all-to-all-start.3 = ((bf16[128,1,4,2048]{3,2,1,0:T(4,128)(2,1)}), bf16[128,1,4,2048]{3,2,1,0:T(4,128)(2,1)}, u32[]{:S(2)}, u32[]{:S(2)}) async-start(bf16[128,1,4,2048]{3,2,1,0:T(4,128)(2,1)} %bitcast.129), calls=%async_computation.3 | async-start | bytes 4194304 | tf_op jit(solution)/shard_map/all_to_all | solution.py:223
  159.3 35.3 %all-to-all-start.1 = ((bf16[128,1,4,2048]{3,2,1,0:T(4,128)(2,1)}), bf16[128,1,4,2048]{3,2,1,0:T(4,128)(2,1)}, u32[]{:S(2)}, u32[]{:S(2)}) async-start(bf16[128,1,4,2048]{3,2,1,0:T(4,128)(2,1)} %bitcast.128), calls=%async_computation.1 | async-start | bytes 4194304 | tf_op jit(solution)/shard_map/all_to_all | solution.py:223
  194.6 35.5 %all-to-all-start.5 = ((bf16[128,1,4,2048]{3,2,1,0:T(4,128)(2,1)}), bf16[128,1,4,2048]{3,2,1,0:T(4,128)(2,1)}, u32[]{:S(2)}, u32[]{:S(2)}) async-start(bf16[128,1,4,2048]{3,2,1,0:T(4,128)(2,1)} %bitcast.123), calls=%async_computation.5 | async-start | bytes 4194304 | tf_op jit(solution)/shard_map/all_to_all | solution.py:223
  230.1 35.3 %all-to-all-start.7 = ((bf16[128,1,4,2048]{3,2,1,0:T(4,128)(2,1)}), bf16[128,1,4,2048]{3,2,1,0:T(4,128)(2,1)}, u32[]{:S(2)}, u32[]{:S(2)}) async-start(bf16[128,1,4,2048]{3,2,1,0:T(4,128)(2,1)} %bitcast.125), calls=%async_computation.7 | async-start | bytes 4194304 | tf_op jit(solution)/shard_map/all_to_all | solution.py:223
  265.4 35.3 %all-to-all-start.4 = ((bf16[128,1,4,2048]{3,2,1,0:T(4,128)(2,1)}), bf16[128,1,4,2048]{3,2,1,0:T(4,128)(2,1)}, u32[]{:S(2)}, u32[]{:S(2)}) async-start(bf16[128,1,4,2048]{3,2,1,0:T(4,128)(2,1)} %bitcast.126), calls=%async_computation.4 | async-start | bytes 4194304 | tf_op jit(solution)/shard_map/all_to_all | solution.py:229
  300.7 35.8 %all-to-all-start.2 = ((bf16[128,1,4,2048]{3,2,1,0:T(4,128)(2,1)}), bf16[128,1,4,2048]{3,2,1,0:T(4,128)(2,1)}, u32[]{:S(2)}, u32[]{:S(2)}) async-start(bf16[128,1,4,2048]{3,2,1,0:T(4,128)(2,1)} %bitcast.127), calls=%async_computation.2 | async-start | bytes 4194304 | tf_op jit(solution)/shard_map/all_to_all | solution.py:229
  336.5 5.1 %copy-start.21 = (f32[1,128,6]{1,0,2:T(1,128)S(1)}, f32[1,128,6]{1,0,2:T(1,128)}, u32[]{:S(2)}) copy-start(f32[1,128,6]{1,0,2:T(1,128)} %param.27) | copy-start | bytes 9220
  336.5 35.5 %all-to-all-start.6 = ((bf16[128,1,4,2048]{3,2,1,0:T(4,128)(2,1)}), bf16[128,1,4,2048]{3,2,1,0:T(4,128)(2,1)}, u32[]{:S(2)}, u32[]{:S(2)}) async-start(bf16[128,1,4,2048]{3,2,1,0:T(4,128)(2,1)} %bitcast.124), calls=%async_computation.6 | async-start | bytes 4194304 | tf_op jit(solution)/shard_map/all_to_all | solution.py:229
  371.9 35.3 %all-to-all-start.8 = ((bf16[128,1,4,2048]{3,2,1,0:T(4,128)(2,1)}), bf16[128,1,4,2048]{3,2,1,0:T(4,128)(2,1)}, u32[]{:S(2)}, u32[]{:S(2)}) async-start(bf16[128,1,4,2048]{3,2,1,0:T(4,128)(2,1)} %bitcast.122), calls=%async_computation.8 | async-start | bytes 4194304 | tf_op jit(solution)/shard_map/all_to_all | solution.py:229
  407.2 2.6 copy-start.5
  407.2 2.6 copy-start.13
  409.8 2.5 copy-start.6
  409.8 2.5 copy-start.12
  412.3 2.5 copy-start.11
  414.7 2.4 copy-start.1
  (3 other events, 3.2 us)
Sparse Core Ops, SparseCore 0:
  28.4 60.8 all-gather.1

commit v5 on v3

--- a/solution.py
+++ b/solution.py
@@ -104,6 +104,17 @@
     copies = jnp.broadcast_to(rows[None], (count,) + rows.shape)
     gathered = lax.all_to_all(copies, axes, split_axis=0, concat_axis=0, tiled=True)
     return gathered.reshape(count * rows.shape[0], rows.shape[1])
+
+
+def ring_gather(rows, axis):
+    size = lax.axis_size(axis)
+    own = lax.axis_index(axis)
+    pieces = [rows]
+    for shift in range(1, size):
+        pairs = [(i, (i + shift) % size) for i in range(size)]
+        pieces.append(lax.ppermute(rows, axis, pairs))
+    sources = (own - jnp.arange(size, dtype=jnp.int32)) % size
+    return jnp.concatenate(pieces, axis=0), sources
 
 
 def on_device(
@@ -154,11 +165,15 @@
         scale_factor,
         latent_width,
     )
-    key_block = lax.all_gather(
-        lax.all_gather(key_rows, "col", axis=0, tiled=True), "row", axis=0, tiled=True
-    )
-    block_member, block_places, block_offsets = token_layout(
-        group_lengths, jnp.int32(0), key_block.shape[0]
+    key_block, col_sources = ring_gather(key_rows, "col")
+    key_block, row_sources = ring_gather(key_block, "row")
+    source_devices = row_sources[:, None] * lax.axis_size("col") + col_sources[None, :]
+    block_places = (
+        source_devices.reshape(-1)[:, None] * token_count
+        + jnp.arange(token_count, dtype=jnp.int32)[None, :]
+    ).reshape(-1)
+    block_member = jnp.sum(
+        (block_places[:, None] >= jnp.cumsum(group_lengths)[None, :]).astype(jnp.int32), axis=1
     )
     visible = (row_member[:, None] == block_member[None, :]) & (
         row_places[:, None] >= block_places[None, :]

time: 378 us -> 391 us (1.034)
  local copies, waits for them, and re-layouts: 17.3 us -> 37.2 us
  blocking collectives: 14.1 us -> 0 us
  between operations: 14.6 us -> 1.52 us
  other arithmetic: 22.6 us -> 30.1 us
  waiting for transfers between devices: 179 us -> 184 us
    ppermute x0 -> x6, waiting for transfers between devices: none -> 16.1 us  [ring_gather(): pieces.append(lax.ppermute(rows, axis, pairs))]
    all_gather x1 -> x0, blocking collectives: 14.1 us -> none  [on_device(): lax.all_gather(key_rows, 'col', axis=0, tiled=True)]
    unnamed x40 -> x67, local copies, waits for them, and re-layouts: 4.2 us -> 16.4 us
    ppermute x0 -> x6, starting transfers between devices: none -> 10.4 us  [ring_gather(): pieces.append(lax.ppermute(rows, axis, pairs))]
    all_to_all x1, waiting for transfers between devices: 9.4 us -> 0.01 us  [gather_rows(): lax.all_to_all(copies, axes, split_axis=0, concat_axis=0, tiled=True)]
    all_to_all x2, starting transfers between devices: 19.7 us -> 15.2 us  [on_device(): lax.all_to_all(outgoing, ('row', 'col', 'rep'), split_axis=0, concat_axis...]
  transfers between devices with their start and end apart: 6 -> 11, of which waited for: 6 -> 6; matrix products, arithmetic and copies ran while one was open for 21% -> 27% of each run, Pallas kernels for 0% -> 0%
where the time goes in v5:
time: 391 us; the launch traced here: 384 us
  waiting for transfers between devices  184 us (47%)
  matrix products  84.5 us (22%)
  starting transfers between devices  46.7 us (12%)
  local copies, waits for them, and re-layouts  37.2 us (10%)
  other arithmetic  30.1 us (8%)
    all_to_all x2, waiting for transfers between devices, on_device(): lax.all_to_all(outgoing, ('row', 'col', 'rep'), split_axis=0, concat_axis...  85.4 us
    all_to_all x2, waiting for transfers between devices, on_device(): lax.all_to_all(produced, ('row', 'col', 'rep'), split_axis=0, concat_axis...  82.5 us
    dot_general x2, matrix products, expert_apply(): joint = jnp.dot(rows, expert_gate_up[0], preferred_element_type=jnp.float32)  20.9 us
    unnamed x67, local copies, waits for them, and re-layouts  16.4 us
    ppermute x6, waiting for transfers between devices, ring_gather(): pieces.append(lax.ppermute(rows, axis, pairs))  16.1 us
    dot_general x2, matrix products, attend_block(): lax.dot_general(query_rows, key_block, (((1,), (1,)), ((), ())), preferre...  15.6 us
    all_to_all x2, starting transfers between devices, on_device(): lax.all_to_all(outgoing, ('row', 'col', 'rep'), split_axis=0, concat_axis...  15.2 us
    all_to_all x2, starting transfers between devices, on_device(): lax.all_to_all(produced, ('row', 'col', 'rep'), split_axis=0, concat_axis...  11.7 us
  transfers between devices with their start and end apart: 11, of which 6 were waited for; matrix products, arithmetic and copies ran while one was open for 27% of the time, Pallas kernels for 0%

profile of v5, /device:TPU:1, one launch (start us, length us, event | category | flops | bytes accessed | tf_op | source)
XLA Modules:
  0.0 384.0 jit_solution(15957130773523525186)
XLA Ops:
  5.6 2.7 fusion.72
  10.5 2.1 collective-permute-start
  12.6 2.6 collective-permute-start.1
  18.1 9.4 %all-to-all-start = ((bf16[128,16,576]{2,1,0:T(8,128)(2,1)}), bf16[128,16,576]{2,1,0:T(8,128)(2,1)}, u32[]{:S(2)}, u32[]{:S(2)}) async-start(bf16[128,16,576]{2,1,0:T(8,128)(2,1)} %broadcast_in_dim.44), calls=%async_computation | async-start | bytes 5242880 | tf_op jit(solution)/shard_map/all_to_all | solution.py:105
  28.1 4.7 %fusion.74 = f32[128,1536]{1,0:T(8,128)} fusion(bf16[2048,1536]{1,0:T(8,128)(2,1)} %param.19, bf16[1,128,2048]{2,1,0:T(8,128)(2,1)S(1)} %copy-done.2, f32[2048]{0:T(1024)S(1)} %convert_element_type.135, f32[128]{0:T(128)} %copy-done.21), kind=kOutput, calls=%fused_computation.90 | convolution fusion | flops 806354944 | bytes 7610880 | tf_op jit(solution)/shard_map/dot_general | solution.py:53
  32.8 2.3 copy.81
  43.5 2.9 fusion.52
  68.3 3.5 collective-permute-start.3
  80.1 4.5 %collective-permute-done.3 = bf16[512,576]{0,1:T(8,128)(2,1)} collective-permute-done((bf16[512,576]{0,1:T(8,128)(2,1)}, bf16[512,576]{0,1:T(8,128)(2,1)}, u32[]{:S(2)}, u32[]{:S(2)}) %collective-permute-start.3) | collective-permute-done | bytes 589856 | tf_op jit(solution)/shard_map/ppermute | solution.py:115
  86.6 11.6 %collective-permute-done.4 = bf16[512,576]{0,1:T(8,128)(2,1)} collective-permute-done((bf16[512,576]{0,1:T(8,128)(2,1)}, bf16[512,576]{0,1:T(8,128)(2,1)}, u32[]{:S(2)}, u32[]{:S(2)}) %collective-permute-start.4) | collective-permute-done | bytes 589856 | tf_op jit(solution)/shard_map/ppermute | solution.py:115
  101.0 9.9 %fusion.91 = (f32[1024]{0:T(1024)S(1)}, f32[1024,2048]{1,0:T(8,128)}) fusion(bf16[2048,576]{0,1:T(8,128)(2,1)} %constant_dynamic-update-slice_fusion, bf16[128,8,576]{2,0,1:T(8,128)(2,1)S(1)} %copy-done.7, s32[2048]{0:T(1024)S(1)} %copy-done.16, s32[1024]{0:T(1024)S(1)} %ge.63, s32[2048]{0:T(1024)S(1)} %convert_reduce_fusion, s32[1024]{0:T(1024)S(1)} %eq.76), kind=kOutput, calls=%fused_computation.142 | convolution fusion | flops 2428500992 | bytes 11956224 | tf_op jit(solution)/shard_map/dot_general | solution.py:75
  110.9 5.8 %multiply_reduce_fusion = (f32[1024]{0:T(1024)S(1)}, f32[1024,2048]{1,0:T(8,128)S(1)}) fusion(bf16[2048,576]{1,0:T(8,128)(2,1)} %bitcast.9, bf16[128,8,576]{2,0,1:T(8,128)(2,1)} %pad_maximum_fusion), kind=kOutput, calls=%fused_computation.3 | convolution fusion | flops 2420112384 | bytes 11931648 | tf_op jit(solution)/shard_map/dot_general | solution.py:75
  118.8 4.2 %fusion.8 = f32[1024,512]{1,0:T(8,128)S(1)} fusion(f32[1024,2048]{1,0:T(8,128)S(1)} %get-tuple-element.27, f32[1024]{0:T(1024)S(1)} %get-tuple-element.21, bf16[2048,576]{1,0:T(8,128)(2,1)} %bitcast.9), kind=kOutput, calls=%fused_computation.12 | convolution fusion | flops 2153775104 | bytes 12587008 | tf_op jit(solution)/shard_map/dot_general | solution.py:85
  124.7 2.6 fusion.68
  130.6 3.3 convert_bitcast_fusion.3
  133.9 9.2 %all-to-all-start.1 = ((bf16[128,1,8,2048]{3,2,1,0:T(8,128)(2,1)}), bf16[128,1,8,2048]{3,2,1,0:T(8,128)(2,1)}, u32[]{:S(2)}, u32[]{:S(2)}) async-start(bf16[128,1,8,2048]{3,2,1,0:T(8,128)(2,1)} %convert_bitcast_fusion.3), calls=%async_computation.1 | async-start | bytes 8388608 | tf_op jit(solution)/shard_map/all_to_all | solution.py:238
  143.1 3.3 convert_bitcast_fusion.1
  146.4 49.0 %all-to-all-done.1 = bf16[128,1,8,2048]{3,2,1,0:T(8,128)(2,1)} async-done(((bf16[128,1,8,2048]{3,2,1,0:T(8,128)(2,1)}), bf16[128,1,8,2048]{3,2,1,0:T(8,128)(2,1)}, u32[]{:S(2)}, u32[]{:S(2)}) %all-to-all-start.1) | async-done | bytes 4194336 | tf_op jit(solution)/shard_map/all_to_all | solution.py:238
  195.4 6.1 %all-to-all-start.3 = ((bf16[128,1,8,2048]{3,2,1,0:T(8,128)(2,1)}), bf16[128,1,8,2048]{3,2,1,0:T(8,128)(2,1)}, u32[]{:S(2)}, u32[]{:S(2)}) async-start(bf16[128,1,8,2048]{3,2,1,0:T(8,128)(2,1)} %convert_bitcast_fusion.1), calls=%async_computation.3 | async-start | bytes 8388608 | tf_op jit(solution)/shard_map/all_to_all | solution.py:238
  201.5 10.4 %fusion.6 = f32[1024,1408]{1,0:T(8,128)S(1)} fusion(bf16[1,2048,1408]{2,1,0:T(8,128)(2,1)} %param.28, bf16[128,1,8,2048]{3,2,1,0:T(8,128)(2,1)} %all-to-all-done.1), kind=kOutput, calls=%fused_computation.10 | convolution fusion | flops 5905580032 | bytes 15728640 | tf_op jit(solution)/shard_map/dot_general | solution.py:96
  211.9 5.2 %convert_bitcast_fusion.2 = bf16[128,1,8,2048]{3,2,1,0:T(8,128)(2,1)} fusion(bf16[1,704,2048]{2,1,0:T(8,128)(2,1)S(1)} %copy-done, f32[1024,1408]{1,0:T(8,128)S(1)} %fusion.6), kind=kOutput, calls=%fused_computation.24 | convolution fusion | flops 2959212544 | bytes 13369344 | tf_op jit(solution)/shard_map/dot_general | solution.py:98
  217.1 36.5 %all-to-all-done.3 = bf16[128,1,8,2048]{3,2,1,0:T(8,128)(2,1)} async-done(((bf16[128,1,8,2048]{3,2,1,0:T(8,128)(2,1)}), bf16[128,1,8,2048]{3,2,1,0:T(8,128)(2,1)}, u32[]{:S(2)}, u32[]{:S(2)}) %all-to-all-start.3) | async-done | bytes 4194336 | tf_op jit(solution)/shard_map/all_to_all | solution.py:238
  253.6 5.6 %all-to-all-start.2 = ((bf16[128,1,8,2048]{3,2,1,0:T(8,128)(2,1)}), bf16[128,1,8,2048]{3,2,1,0:T(8,128)(2,1)}, u32[]{:S(2)}, u32[]{:S(2)}) async-start(bf16[128,1,8,2048]{3,2,1,0:T(8,128)(2,1)} %convert_bitcast_fusion.2), calls=%async_computation.2 | async-start | bytes 8388608 | tf_op jit(solution)/shard_map/all_to_all | solution.py:244
  259.2 10.4 %fusion.4 = f32[1024,1408]{1,0:T(8,128)S(1)} fusion(bf16[1,2048,1408]{2,1,0:T(8,128)(2,1)} %param.28, bf16[128,1,8,2048]{3,2,1,0:T(8,128)(2,1)} %all-to-all-done.3), kind=kOutput, calls=%fused_computation.8 | convolution fusion | flops 5905580032 | bytes 15728640 | tf_op jit(solution)/shard_map/dot_general | solution.py:96
  269.6 5.2 %convert_bitcast_fusion = bf16[128,1,8,2048]{3,2,1,0:T(8,128)(2,1)} fusion(bf16[1,704,2048]{2,1,0:T(8,128)(2,1)S(1)} %copy-done, f32[1024,1408]{1,0:T(8,128)S(1)} %fusion.4), kind=kOutput, calls=%fused_computation.21 | convolution fusion | flops 2959212544 | bytes 13369344 | tf_op jit(solution)/shard_map/dot_general | solution.py:98
  274.9 36.6 %all-to-all-done.2 = bf16[128,1,8,2048]{3,2,1,0:T(8,128)(2,1)} async-done(((bf16[128,1,8,2048]{3,2,1,0:T(8,128)(2,1)}), bf16[128,1,8,2048]{3,2,1,0:T(8,128)(2,1)}, u32[]{:S(2)}, u32[]{:S(2)}) %all-to-all-start.2) | async-done | bytes 4194336 | tf_op jit(solution)/shard_map/all_to_all | solution.py:244
  311.5 6.1 %all-to-all-start.4 = ((bf16[128,1,8,2048]{3,2,1,0:T(8,128)(2,1)}), bf16[128,1,8,2048]{3,2,1,0:T(8,128)(2,1)}, u32[]{:S(2)}, u32[]{:S(2)}) async-start(bf16[128,1,8,2048]{3,2,1,0:T(8,128)(2,1)} %convert_bitcast_fusion), calls=%async_computation.4 | async-start | bytes 8388608 | tf_op jit(solution)/shard_map/all_to_all | solution.py:244
  318.9 5.0 %add_bitcast_fusion.1 = f32[64,8,2048]{2,1,0:T(8,128)} fusion(bf16[64,2,8,2048]{3,2,1,0:T(8,128)(2,1)} %bitcast.25), kind=kLoop, calls=%fused_computation.23 | loop fusion | flops 3145728 | bytes 8388608 | tf_op jit(solution)/shard_map/add | solution.py:247
  323.9 45.8 %all-to-all-done.4 = bf16[128,1,8,2048]{3,2,1,0:T(8,128)(2,1)} async-done(((bf16[128,1,8,2048]{3,2,1,0:T(8,128)(2,1)}), bf16[128,1,8,2048]{3,2,1,0:T(8,128)(2,1)}, u32[]{:S(2)}, u32[]{:S(2)}) %all-to-all-start.4) | async-done | bytes 4194336 | tf_op jit(solution)/shard_map/all_to_all | solution.py:244
  369.7 3.2 add_bitcast_fusion
  373.2 4.7 %fusion.26 = f32[128,2048]{1,0:T(8,128)S(1)} fusion(f32[64,8,2048]{2,1,0:T(8,128)S(1)} %copy-done.1, f32[128,64,8]{0,2,1:T(8,128)S(1)} %copy-done.10), kind=kOutput, calls=%fused_computation.39 | convolution fusion | flops 1610612736 | bytes 5505024 | tf_op jit(solution)/shard_map/dot_general | solution.py:248
  378.0 5.6 %fusion.42 = bf16[1,128,2048]{2,1,0:T(8,128)(2,1)} fusion(f32[128,2048]{1,0:T(8,128)S(1)} %fusion.26, f32[64,8,2048]{2,1,0:T(8,128)S(1)} %add_bitcast_fusion, bf16[128,2048]{1,0:T(8,128)(2,1)S(1)} %copy-done.4, f32[128,64,8]{0,2,1:T(8,128)S(1)} %copy-done.9), kind=kOutput, calls=%fused_computation.46 | convolution fusion | flops 1611661312 | bytes 6553600 | tf_op jit(solution)/shard_map/dot_general | solution.py:248
  (131 shorter events, 62.5 us)
Async XLA Ops:
  0.6 211.3 %copy-start = (bf16[1,704,2048]{2,1,0:T(8,128)(2,1)S(1)}, bf16[1,704,2048]{2,1,0:T(8,128)(2,1)}, u32[]{:S(2)}) copy-start(bf16[1,704,2048]{2,1,0:T(8,128)(2,1)} %param.29) | copy-start | bytes 8650756
  0.6 15.6 %copy-start.17 = (bf16[16,576]{1,0:T(8,128)(2,1)S(1)}, bf16[16,576]{1,0:T(8,128)(2,1)}, u32[]{:S(2)}) copy-start(bf16[16,576]{1,0:T(8,128)(2,1)} %param.17) | copy-start | bytes 55300
  4.9 11.4 %copy-start.21 = (f32[128]{0:T(128)}, f32[128]{0:T(128)S(1)}, u32[]{:S(2)}) copy-start(f32[128]{0:T(128)S(1)} %add_rsqrt_fusion.2) | copy-start | bytes 1540
  10.5 55.8 %collective-permute-start = (bf16[128,576]{0,1:T(8,128)(2,1)}, bf16[128,576]{0,1:T(8,128)(2,1)}, u32[]{:S(2)}, u32[]{:S(2)}) collective-permute-start(bf16[128,576]{0,1:T(8,128)(2,1)} %get-tuple-element.17), channel_id=1, source_target_pairs={{0,8},{8,16},{16,24},{24,0},{1,9},{9,17},{17,25},{25,1},{2,10},{10... | collective-permute-start | bytes 442376 | tf_op jit(solution)/shard_map/ppermute | solution.py:115
  12.6 53.7 %collective-permute-start.1 = (bf16[128,576]{0,1:T(8,128)(2,1)}, bf16[128,576]{0,1:T(8,128)(2,1)}, u32[]{:S(2)}, u32[]{:S(2)}) collective-permute-start(bf16[128,576]{0,1:T(8,128)(2,1)} %get-tuple-element.17), channel_id=1, source_target_pairs={{0,16},{8,24},{16,0},{24,8},{1,17},{9,25},{17,1},{25,9},{2,18},{10... | collective-permute-start | bytes 442376 | tf_op jit(solution)/shard_map/ppermute | solution.py:115
  15.2 51.1 %collective-permute-start.2 = (bf16[128,576]{0,1:T(8,128)(2,1)}, bf16[128,576]{0,1:T(8,128)(2,1)}, u32[]{:S(2)}, u32[]{:S(2)}) collective-permute-start(bf16[128,576]{0,1:T(8,128)(2,1)} %get-tuple-element.17), channel_id=1, source_target_pairs={{0,24},{8,0},{16,8},{24,16},{1,25},{9,1},{17,9},{25,17},{2,26},{10... | collective-permute-start | bytes 442376 | tf_op jit(solution)/shard_map/ppermute | solution.py:115
  18.1 10.0 %copy-start.2 = (bf16[1,128,2048]{2,1,0:T(8,128)(2,1)S(1)}, bf16[1,128,2048]{2,1,0:T(8,128)(2,1)}, u32[]{:S(2)}) copy-start(bf16[1,128,2048]{2,1,0:T(8,128)(2,1)} %param.15) | copy-start | bytes 1572868
  18.1 92.8 %all-to-all-start = ((bf16[128,16,576]{2,1,0:T(8,128)(2,1)}), bf16[128,16,576]{2,1,0:T(8,128)(2,1)}, u32[]{:S(2)}, u32[]{:S(2)}) async-start(bf16[128,16,576]{2,1,0:T(8,128)(2,1)} %broadcast_in_dim.44), calls=%async_computation | async-start | bytes 5242880 | tf_op jit(solution)/shard_map/all_to_all | solution.py:105
  43.5 22.8 %copy-start.14 = (bf16[128,32]{0,1:T(8,128)(2,1)S(1)}, bf16[128,32]{0,1:T(8,128)(2,1)}, u32[]{:S(2)}) copy-start(bf16[128,32]{0,1:T(8,128)(2,1)} %copy-done.13) | copy-start | bytes 24580
  61.8 10.5 %copy-start.6 = (bf16[128,8,512]{2,0,1:T(8,128)(2,1)S(1)}, bf16[128,8,512]{2,0,1:T(8,128)(2,1)}, u32[]{:S(2)}) copy-start(bf16[128,8,512]{2,0,1:T(8,128)(2,1)} %fusion.52) | copy-start | bytes 3145732
  61.8 11.7 %copy-start.24 = (s32[128]{0:T(128)S(1)}, s32[128]{0:T(128)}, u32[]{:S(2)}) copy-start(s32[128]{0:T(128)} %copy-done.23) | copy-start | bytes 1540
  68.3 6.2 %copy-start.19 = (bf16[2048]{0:T(1024)(128)(2,1)S(1)}, bf16[2048]{0:T(1024)(128)(2,1)}, u32[]{:S(2)}) copy-start(bf16[2048]{0:T(1024)(128)(2,1)} %param.25) | copy-start | bytes 12292
  68.3 6.2 %copy-start.16 = (s32[2048]{0:T(1024)S(1)}, s32[2048]{0:T(1024)}, u32[]{:S(2)}) copy-start(s32[2048]{0:T(1024)} %add_bitcast_fusion.2) | copy-start | bytes 24580
  68.3 6.3 %copy-start.26 = (s32[4,1]{0,1:T(1,128)S(1)}, s32[4,1]{0,1:T(1,128)}, u32[]{:S(2)}) copy-start(s32[4,1]{0,1:T(1,128)} %copy-done.25) | copy-start | bytes 52
  68.3 16.3 %collective-permute-start.3 = (bf16[512,576]{0,1:T(8,128)(2,1)}, bf16[512,576]{0,1:T(8,128)(2,1)}, u32[]{:S(2)}, u32[]{:S(2)}) collective-permute-start(bf16[512,576]{0,1:T(8,128)(2,1)} %pad_maximum_fusion.1), channel_id=1, source_target_pairs={{0,32},{32,64},{64,96},{96,0},{1,33},{33,65},{65,97},{97,1},{2,34}... | collective-permute-start | bytes 1769480 | tf_op jit(solution)/shard_map/ppermute | solution.py:115
  71.8 26.3 %collective-permute-start.4 = (bf16[512,576]{0,1:T(8,128)(2,1)}, bf16[512,576]{0,1:T(8,128)(2,1)}, u32[]{:S(2)}, u32[]{:S(2)}) collective-permute-start(bf16[512,576]{0,1:T(8,128)(2,1)} %pad_maximum_fusion.1), channel_id=1, source_target_pairs={{0,64},{32,96},{64,0},{96,32},{1,65},{33,97},{65,1},{97,33},{2,66}... | collective-permute-start | bytes 1769480 | tf_op jit(solution)/shard_map/ppermute | solution.py:115
  74.5 26.5 %copy-start.7 = (bf16[128,8,576]{2,0,1:T(8,128)(2,1)S(1)}, bf16[128,8,576]{2,0,1:T(8,128)(2,1)}, u32[]{:S(2)}) copy-start(bf16[128,8,576]{2,0,1:T(8,128)(2,1)} %pad_maximum_fusion) | copy-start | bytes 3538948
  74.7 25.5 %collective-permute-start.5 = (bf16[512,576]{0,1:T(8,128)(2,1)}, bf16[512,576]{0,1:T(8,128)(2,1)S(1)}, u32[]{:S(2)}, u32[]{:S(2)}) collective-permute-start(bf16[512,576]{0,1:T(8,128)(2,1)} %pad_maximum_fusion.1), channel_id=1, source_target_pairs={{0,96},{32,0},{64,32},{96,64},{1,97},{33,1},{65,33},{97,65},{2,98}... | collective-permute-start | bytes 1769480 | tf_op jit(solution)/shard_map/ppermute | solution.py:115
  116.7 6.3 %slice-start = ((s8[8388608]{0:T(1024)(128)(4,1)}), s8[4194304]{0:T(1024)(128)(4,1)S(1)}, s32[]{:S(2)}) async-start(s8[8388608]{0:T(1024)(128)(4,1)} %bitcast.108), calls=%async_computation.5 | async-start | bytes 8388608
  118.8 4.2 %slice-start.1 = ((s8[8388608]{0:T(1024)(128)(4,1)}), s8[4194304]{0:T(1024)(128)(4,1)S(1)}, s32[]{:S(2)}) async-start(s8[8388608]{0:T(1024)(128)(4,1)} %bitcast.108), calls=%async_computation.6 | async-start | bytes 8388608
  124.7 3.5 copy-start.5
  133.9 9.2 %copy-start.11 = (bf16[128,64,8]{0,2,1:T(8,128)(2,1)S(1)}, bf16[128,64,8]{0,2,1:T(8,128)(2,1)}, u32[]{:S(2)}) copy-start(bf16[128,64,8]{0,2,1:T(8,128)(2,1)} %get-tuple-element.15) | copy-start | bytes 393220
  133.9 9.2 %copy-start.4 = (bf16[128,2048]{1,0:T(8,128)(2,1)S(1)}, bf16[128,2048]{1,0:T(8,128)(2,1)}, u32[]{:S(2)}) copy-start(bf16[128,2048]{1,0:T(8,128)(2,1)} %copy-done.3) | copy-start | bytes 1572868
  133.9 61.5 %all-to-all-start.1 = ((bf16[128,1,8,2048]{3,2,1,0:T(8,128)(2,1)}), bf16[128,1,8,2048]{3,2,1,0:T(8,128)(2,1)}, u32[]{:S(2)}, u32[]{:S(2)}) async-start(bf16[128,1,8,2048]{3,2,1,0:T(8,128)(2,1)} %convert_bitcast_fusion.3), calls=%async_computation.1 | async-start | bytes 8388608 | tf_op jit(solution)/shard_map/all_to_all | solution.py:238
  195.4 58.2 %all-to-all-start.3 = ((bf16[128,1,8,2048]{3,2,1,0:T(8,128)(2,1)}), bf16[128,1,8,2048]{3,2,1,0:T(8,128)(2,1)}, u32[]{:S(2)}, u32[]{:S(2)}) async-start(bf16[128,1,8,2048]{3,2,1,0:T(8,128)(2,1)} %convert_bitcast_fusion.1), calls=%async_computation.3 | async-start | bytes 8388608 | tf_op jit(solution)/shard_map/all_to_all | solution.py:238
  253.6 57.9 %all-to-all-start.2 = ((bf16[128,1,8,2048]{3,2,1,0:T(8,128)(2,1)}), bf16[128,1,8,2048]{3,2,1,0:T(8,128)(2,1)}, u32[]{:S(2)}, u32[]{:S(2)}) async-start(bf16[128,1,8,2048]{3,2,1,0:T(8,128)(2,1)} %convert_bitcast_fusion.2), calls=%async_computation.2 | async-start | bytes 8388608 | tf_op jit(solution)/shard_map/all_to_all | solution.py:244
  274.9 42.7 %copy-start.20 = (f32[1,128,6]{1,0,2:T(1,128)S(1)}, f32[1,128,6]{1,0,2:T(1,128)}, u32[]{:S(2)}) copy-start(f32[1,128,6]{1,0,2:T(1,128)} %param.27) | copy-start | bytes 9220
  274.9 42.8 %copy-start.15 = (s32[128,6]{0,1:T(8,128)S(1)}, s32[128,6]{0,1:T(8,128)}, u32[]{:S(2)}) copy-start(s32[128,6]{0,1:T(8,128)} %copy.92) | copy-start | bytes 9220
  311.5 58.2 %all-to-all-start.4 = ((bf16[128,1,8,2048]{3,2,1,0:T(8,128)(2,1)}), bf16[128,1,8,2048]{3,2,1,0:T(8,128)(2,1)}, u32[]{:S(2)}, u32[]{:S(2)}) async-start(bf16[128,1,8,2048]{3,2,1,0:T(8,128)(2,1)} %convert_bitcast_fusion), calls=%async_computation.4 | async-start | bytes 8388608 | tf_op jit(solution)/shard_map/all_to_all | solution.py:244
  369.7 3.4 copy-start.1
  369.7 3.5 copy-start.10
  372.9 5.0 %copy-start.9 = (f32[128,64,8]{0,2,1:T(8,128)S(1)}, f32[128,64,8]{0,2,1:T(8,128)}, u32[]{:S(2)}) copy-start(f32[128,64,8]{0,2,1:T(8,128)} %get-tuple-element.11) | copy-start | bytes 786436
  (8 other events, 9.7 us)
